TPU v7x, 512 devices: a whole 4x4x16 slice. The times are simulated.
512 devices in a mesh: dp: 64 (over z, x_lo, core), tensor: 8 (over y, x_hi).
Axes of the slice: x: 4 (x_hi: 2, x_lo: 2; x = x_hi * 2 + x_lo), y: 4, z: 16, core: 2. Of those that a mesh axis runs over, the one named last changes fastest.
Arguments:
- hidden_in: bfloat16 [16384, 4096], P(('dp', 'tensor')), may hold values from -12 to 12
- norm_gain: bfloat16 [4096], replicated, may hold values from 0.5 to 1.5
- w_query: bfloat16 [4096, 4096], P('dp', 'tensor'), may hold values from -0.11328125 to 0.11328125
- w_key: bfloat16 [4096, 1024], P('dp', 'tensor'), may hold values from -0.11328125 to 0.11328125
- w_value: bfloat16 [4096, 1024], P('dp', 'tensor'), may hold values from -0.09375 to 0.09375
- w_out: bfloat16 [4096, 4096], P('tensor', 'dp'), may hold values from -0.09375 to 0.09375
- segment: int32 [16384], P('dp'), may hold values from -1 to 1, as said below
Outputs:
- hidden_out: bfloat16 [16384, 4096], P(('dp', 'tensor'))
- kv_cache: bfloat16 [16384, 8, 256], P('dp', 'tensor')
Inputs may be any that keep to these rules, and one draw needn't show every extreme that they name: `segment`: within each pack of 256 rows, prompts are numbered from 0 in order and each starts at a multiple of 128; a prompt's last tile may end in rows of -1, and whole tiles of -1 may only follow the last prompt of a pack; the first tile of every pack holds a prompt; in every draw some pack has no tile of -1 only and holds one prompt a tile.
All inputs are finite; a program needn't handle non-finite values.
Results may differ from a plain program's by a relative error of at most 0.0085.
Values may be sent and summed in bfloat16 or wider, within the bound.
No kernel may reach another device: no remote copies, remote signals or barrier semaphores. Data moves between devices by JAX's collectives and lax.ppermute only.
A program may use at most 64 MiB of HBM per device.

v0:
```python
import jax
import jax.numpy as jnp
from jax import lax
from jax.sharding import PartitionSpec as P

HEAD = 128


rope_theta = 500000.0
norm_epsilon = 1e-05


def inverse_frequency(head_width):
    exponent = jnp.arange(0, head_width, 2).astype(jnp.float32) / head_width
    base_freq = rope_theta ** (-exponent)
    wavelength = 2.0 * jnp.pi / base_freq
    smooth = (8192.0 / wavelength - 1.0) / 3.0
    blended = (1.0 - smooth) * base_freq / 8.0 + smooth * base_freq
    return jnp.where(
        wavelength < 2048.0, base_freq, jnp.where(wavelength > 8192.0, base_freq / 8.0, blended)
    )


def positions_of(segment):
    row_index = jnp.arange(segment.shape[0], dtype=jnp.int32)
    changed = jnp.concatenate([jnp.ones((1,), dtype=bool), segment[1:] != segment[:-1]])
    begins = lax.cummax(jnp.where(changed, row_index, 0), axis=0)
    return row_index - begins


def rotate(vectors, position):
    head_width = vectors.shape[-1]
    half_width = head_width // 2
    angles = position.astype(jnp.float32)[:, None] * inverse_frequency(head_width)[None, :]
    cosine = jnp.concatenate([jnp.cos(angles), jnp.cos(angles)], axis=-1)[:, None, :]
    sine_table = jnp.concatenate([jnp.sin(angles), jnp.sin(angles)], axis=-1)[:, None, :]
    turned = jnp.concatenate([-vectors[..., half_width:], vectors[..., :half_width]], axis=-1)
    return vectors * cosine + turned * sine_table


def rms_normed(rows_float, norm_gain):
    mean_square = jnp.mean(rows_float * rows_float, axis=-1, keepdims=True)
    return (
        rows_float * lax.rsqrt(mean_square + norm_epsilon) * norm_gain.astype(jnp.float32)
    ).astype(jnp.bfloat16)


def visible_pairs(segment, key_count):
    row_index = jnp.arange(segment.shape[0], dtype=jnp.int32)
    key_index = jnp.arange(key_count, dtype=jnp.int32)
    same_segment = (segment[:, None] == segment[None, :]) & (segment[:, None] >= 0)
    causal = key_index[None, :] <= row_index[:, None]
    return same_segment & causal | (key_index[None, :] == row_index[:, None])


def body(hidden_in, norm_gain, w_query, w_key, w_value, w_out, segment):
    pack_rows = segment.shape[0]
    query_cols = w_query.shape[1]
    kv_cols = w_key.shape[1]
    query_heads = query_cols // HEAD
    kv_heads = kv_cols // HEAD
    group_size = query_heads // kv_heads
    score_scale = HEAD ** (-0.5)
    rows_float = hidden_in.astype(jnp.float32)
    normed = rms_normed(rows_float, norm_gain)
    gathered = lax.all_gather(normed, "tensor", axis=0, tiled=True)
    joined = jnp.concatenate(
        (
            lax.all_gather(w_query, "dp", axis=0, tiled=True),
            lax.all_gather(w_key, "dp", axis=0, tiled=True),
            lax.all_gather(w_value, "dp", axis=0, tiled=True),
        ),
        axis=1,
    )
    projected = jnp.dot(gathered, joined, preferred_element_type=jnp.float32)
    position = positions_of(segment)
    query_rows = rotate(
        projected[:, :query_cols].reshape(pack_rows, query_heads, HEAD), position
    ).astype(jnp.bfloat16)
    key_rows = rotate(
        projected[:, query_cols : query_cols + kv_cols].reshape(pack_rows, kv_heads, HEAD), position
    ).astype(jnp.bfloat16)
    value_rows = (
        projected[:, query_cols + kv_cols :].astype(jnp.bfloat16).reshape(pack_rows, kv_heads, HEAD)
    )
    cache_rows = jnp.concatenate([key_rows, value_rows], axis=-1)
    grouped_query = query_rows.reshape(pack_rows, kv_heads, group_size, HEAD)
    scores = (
        jnp.einsum("skgh,tkh->kgst", grouped_query, key_rows, preferred_element_type=jnp.float32)
        * score_scale
    )
    allowed = visible_pairs(segment, pack_rows)
    scores = jnp.where(allowed, scores, -1e30)
    row_max = jnp.max(scores, axis=-1, keepdims=True)
    weight = jnp.exp(scores - row_max)
    weight_sum = jnp.sum(weight, axis=-1)
    mixed_rows = (
        jnp.einsum(
            "kgst,tkh->kgsh",
            weight.astype(jnp.bfloat16),
            value_rows,
            preferred_element_type=jnp.float32,
        )
        / weight_sum[..., None]
    )
    attended = (
        jnp.transpose(mixed_rows, (2, 0, 1, 3)).astype(jnp.bfloat16).reshape(pack_rows, query_cols)
    )
    out_full = lax.all_gather(w_out, "dp", axis=1, tiled=True)
    summed = lax.psum_scatter(
        jnp.dot(attended, out_full, preferred_element_type=jnp.float32).astype(jnp.bfloat16),
        "tensor",
        scatter_dimension=0,
        tiled=True,
    ).astype(jnp.float32)
    hidden_out = (summed + rows_float).astype(jnp.bfloat16)
    return (hidden_out, cache_rows)


def solution(mesh):
    return jax.shard_map(
        body,
        mesh=mesh,
        in_specs=(
            P(("dp", "tensor"), None),
            P(),
            P("dp", "tensor"),
            P("dp", "tensor"),
            P("dp", "tensor"),
            P("tensor", "dp"),
            P("dp"),
        ),
        out_specs=(P(("dp", "tensor"), None), P("dp", "tensor", None)),
        check_vma=False,
    )
```

profile of v0, /device:TPU:1, one launch (start us, length us, event | category | flops | bytes accessed | tf_op | source)
XLA Modules:
  0.0 671.4 jit_solution(11263055543441471757)
XLA Ops:
  7.2 0.7 all-gather.10.cloned.1.call-update
  7.9 0.7 all-gather.12.cloned.1.call-update
  8.7 0.7 convert_element_type.62
  9.4 1.1 fusion.11
  10.5 1.8 fusion.13
  12.4 0.5 all-gather.8.cloned.1.call-update
  13.0 0.5 all-gather.14.cloned.1.call-update
  13.5 0.8 slice_compare_fusion
  15.0 0.7 broadcast_compare_fusion
  15.8 0.9 fusion.23
  16.6 0.5 multiply_cosine_fusion
  17.2 119.8 %all-gather.10.cloned.1.call-done = bf16[4096,128]{1,0:T(8,128)(2,1)} async-done(((bf16[64,128]{1,0:T(8,128)(2,1)}), bf16[4096,128]{1,0:T(8,128)(2,1)}) %all-gather.10.cloned.1.call-update) | async-done | bytes 1048592 | tf_op jit(solution)/shard_map/all_gather | solution.py:70
  137.0 119.9 %all-gather.12.cloned.1.call-done = bf16[4096,128]{1,0:T(8,128)(2,1)} async-done(((bf16[64,128]{1,0:T(8,128)(2,1)}), bf16[4096,128]{1,0:T(8,128)(2,1)}) %all-gather.12.cloned.1.call-update) | async-done | bytes 1048592 | tf_op jit(solution)/shard_map/all_gather | solution.py:71
  256.9 68.1 %all-gather.6.cloned.1.call-done = bf16[256,4096]{1,0:T(8,128)(2,1)} async-done(((bf16[32,4096]{1,0:T(8,128)(2,1)}), bf16[256,4096]{1,0:T(8,128)(2,1)}) %all-gather.6.cloned.1.call-update) | async-done | bytes 2097168 | tf_op jit(solution)/shard_map/all_gather | solution.py:66
  325.0 124.9 %all-gather.8.cloned.1.call-done = bf16[4096,512]{1,0:T(8,128)(2,1)} async-done(((bf16[64,512]{1,0:T(8,128)(2,1)}), bf16[4096,512]{1,0:T(8,128)(2,1)}) %all-gather.8.cloned.1.call-update) | async-done | bytes 4194320 | tf_op jit(solution)/shard_map/all_gather | solution.py:69
  449.8 5.3 fusion
  455.7 0.3 slice_negate_fusion
  456.0 0.4 maximum_multiply_fusion
  456.4 0.4 fusion.33
  457.3 114.6 %all-gather.14.cloned.1.call-done = bf16[512,4096]{0,1:T(8,128)(2,1)} async-done(((bf16[512,64]{0,1:T(8,128)(2,1)}), bf16[512,4096]{0,1:T(8,128)(2,1)}) %all-gather.14.cloned.1.call-update) | async-done | bytes 4194320 | tf_op jit(solution)/shard_map/all_gather | solution.py:109
  571.9 4.9 convolution_convert_fusion
  576.8 0.7 pad_maximum_fusion.2
  577.4 85.4 %reduce-scatter.2.cloned.1.call-done = bf16[32,4096]{1,0:T(8,128)(2,1)} async-done(((bf16[256,4096]{1,0:T(8,128)(2,1)}), bf16[32,4096]{1,0:T(8,128)(2,1)}) %reduce-scatter.2.cloned.1.call-update) | async-done | bytes 262160 | tf_op jit(solution)/shard_map/reduce_scatter | solution.py:110
  662.9 1.7 fusion.14
  (27 shorter events, 2.1 us)
Async XLA Ops:
  7.2 129.8 %all-gather.10.cloned.1.call-start = ((), (), s32[]{:S(2)}) async-start(), calls=%async_computation.3 | async-start | bytes 1064960 | tf_op jit(solution)/shard_map/all_gather | solution.py:70
  7.9 249.0 %all-gather.12.cloned.1.call-start = ((), (), s32[]{:S(2)}) async-start(), calls=%async_computation.4 | async-start | bytes 1064960 | tf_op jit(solution)/shard_map/all_gather | solution.py:71
  8.6 316.3 %all-gather.6.cloned.1.call-start = ((), (), s32[]{:S(2)}) async-start(), calls=%async_computation.1 | async-start | bytes 2359296 | tf_op jit(solution)/shard_map/all_gather | solution.py:66
  12.3 437.5 %all-gather.8.cloned.1.call-start = ((), (), s32[]{:S(2)}) async-start(), calls=%async_computation.2 | async-start | bytes 4259840 | tf_op jit(solution)/shard_map/all_gather | solution.py:69
  12.9 559.0 %all-gather.14.cloned.1.call-start = ((), (), s32[]{:S(2)}) async-start(), calls=%async_computation.5 | async-start | bytes 4259840 | tf_op jit(solution)/shard_map/all_gather | solution.py:109
  13.5 649.4 %reduce-scatter.2.cloned.1.call-start = ((), (), s32[]{:S(2)}) async-start(), calls=%async_computation.6 | async-start | bytes 2359296 | tf_op jit(solution)/shard_map/reduce_scatter | solution.py:110
  571.9 91.0 %copy-start = (bf16[32,4096]{1,0:T(8,128)(2,1)S(1)}, bf16[32,4096]{1,0:T(8,128)(2,1)}, u32[]{:S(2)}) copy-start(bf16[32,4096]{1,0:T(8,128)(2,1)} %param.7) | copy-start | bytes 786436
Sparse Core Ops, SparseCore 0:
  10.1 126.8 all-gather.9
  139.1 117.6 all-gather.11
  260.7 64.2 all-gather.5
  327.0 122.8 all-gather.7
  451.8 119.9 all-gather.13
  576.9 85.9 reduce-scatter.1
where the time goes:
time: 672 us; the launch traced here: 671 us
  waiting for transfers between devices  635 us (94%)
  between operations  14.2 us (2%)
  matrix products  10.8 us (2%)
  other arithmetic  10.6 us (2%)
    all_gather x1, waiting for transfers between devices, body(): lax.all_gather(w_query, 'dp', axis=0, tiled=True)  125 us
    all_gather x1, waiting for transfers between devices, body(): lax.all_gather(w_value, 'dp', axis=0, tiled=True)  120 us
    all_gather x1, waiting for transfers between devices, body(): lax.all_gather(w_key, 'dp', axis=0, tiled=True)  120 us
    all_gather x1, waiting for transfers between devices, body(): out_full = lax.all_gather(w_out, 'dp', axis=1, tiled=True)  115 us
    reduce_scatter x1, waiting for transfers between devices, body(): lax.psum_scatter(jnp.dot(attended, out_full, preferred_element_type=jnp.f...  85.4 us
    all_gather x1, waiting for transfers between devices, body(): gathered = lax.all_gather(normed, 'tensor', axis=0, tiled=True)  68.1 us
  transfers between devices with their start and end apart: 6, of which 6 were waited for; matrix products, arithmetic and copies ran while one was open for 2% of the time, Pallas kernels for 0%

commit v1 on v0

--- a/solution.py
+++ b/solution.py
@@ -64,14 +64,10 @@
     rows_float = hidden_in.astype(jnp.float32)
     normed = rms_normed(rows_float, norm_gain)
     gathered = lax.all_gather(normed, "tensor", axis=0, tiled=True)
-    joined = jnp.concatenate(
-        (
-            lax.all_gather(w_query, "dp", axis=0, tiled=True),
-            lax.all_gather(w_key, "dp", axis=0, tiled=True),
-            lax.all_gather(w_value, "dp", axis=0, tiled=True),
-        ),
-        axis=1,
-    )
+    packed = jnp.concatenate((w_query, w_key, w_value, w_out.T), axis=1)
+    packed_full = lax.all_gather(packed, "dp", axis=0, tiled=True)
+    joined = packed_full[:, : query_cols + 2 * kv_cols]
+    out_full_t = packed_full[:, query_cols + 2 * kv_cols :]
     projected = jnp.dot(gathered, joined, preferred_element_type=jnp.float32)
     position = positions_of(segment)
     query_rows = rotate(
@@ -106,9 +102,11 @@
     attended = (
         jnp.transpose(mixed_rows, (2, 0, 1, 3)).astype(jnp.bfloat16).reshape(pack_rows, query_cols)
     )
-    out_full = lax.all_gather(w_out, "dp", axis=1, tiled=True)
+    out_rows = lax.dot_general(
+        attended, out_full_t, (((1,), (1,)), ((), ())), preferred_element_type=jnp.float32
+    )
     summed = lax.psum_scatter(
-        jnp.dot(attended, out_full, preferred_element_type=jnp.float32).astype(jnp.bfloat16),
+        out_rows.astype(jnp.bfloat16),
         "tensor",
         scatter_dimension=0,
         tiled=True,

time: 672 us -> 325 us (0.48)
  waiting for transfers between devices: 635 us -> 287 us
    all_gather x4 -> x1, waiting for transfers between devices: 479 us -> 132 us  [body(): packed_full = lax.all_gather(packed, 'dp', axis=0, tiled=True)]
  transfers between devices with their start and end apart: 6 -> 3, of which waited for: 6 -> 3; matrix products, arithmetic and copies ran while one was open for 2% -> 2% of each run, Pallas kernels for 0% -> 0%
where the time goes in v1:
time: 325 us; the launch traced here: 324 us
  waiting for transfers between devices  287 us (88%)
  between operations  13.9 us (4%)
  other arithmetic  12.2 us (4%)
  matrix products  10.7 us (3%)
    all_gather x1, waiting for transfers between devices, body(): packed_full = lax.all_gather(packed, 'dp', axis=0, tiled=True)  132 us
    reduce_scatter x1, waiting for transfers between devices, body(): lax.psum_scatter(out_rows.astype(jnp.bfloat16), 'tensor', scatter_dimensi...  85.7 us
    all_gather x1, waiting for transfers between devices, body(): gathered = lax.all_gather(normed, 'tensor', axis=0, tiled=True)  69 us
  transfers between devices with their start and end apart: 3, of which 3 were waited for; matrix products, arithmetic and copies ran while one was open for 2% of the time, Pallas kernels for 0%

profile of v1, /device:TPU:1, one launch (start us, length us, event | category | flops | bytes accessed | tf_op | source)
XLA Modules:
  0.0 324.2 jit_solution(5940702748861386744)
XLA Ops:
  7.2 0.7 convert_element_type.62
  7.9 1.1 fusion.8
  9.0 1.8 fusion.10
  10.9 1.6 pad_maximum_fusion
  12.6 0.8 slice_compare_fusion
  13.5 0.3 reduce-window.9
  13.9 0.1 slice_reduce_fusion
  14.0 0.7 broadcast_compare_fusion
  14.8 0.9 fusion.20
  15.7 0.5 multiply_cosine_fusion
  16.2 69.0 %all-gather.3.cloned.1.call-done = bf16[256,4096]{1,0:T(8,128)(2,1)} async-done(((bf16[32,4096]{1,0:T(8,128)(2,1)}), bf16[256,4096]{1,0:T(8,128)(2,1)}) %all-gather.3.cloned.1.call-update) | async-done | bytes 2097168 | tf_op jit(solution)/shard_map/all_gather | solution.py:66
  85.2 132.1 %all-gather.5.cloned.1.call-done = bf16[4096,1280]{1,0:T(8,128)(2,1)} async-done(((bf16[64,1280]{1,0:T(8,128)(2,1)}), bf16[4096,1280]{1,0:T(8,128)(2,1)}) %all-gather.5.cloned.1.call-update) | async-done | bytes 10485776 | tf_op jit(solution)/shard_map/all_gather | solution.py:68
  217.3 5.2 %fusion = f32[256,768]{1,0:T(8,128)S(1)} fusion(bf16[256,4096]{1,0:T(8,128)(2,1)} %all-gather.3.cloned.1.call-done, bf16[4096,1280]{1,0:T(8,128)(2,1)} %all-gather.5.cloned.1.call-done), kind=kOutput, calls=%fused_computation | convolution fusion | flops 1610612736 | bytes 9175040 | tf_op jit(solution)/shard_map/dot_general | solution.py:71
  222.7 0.2 reshape.129
  222.9 0.3 slice_negate_fusion
  223.2 0.2 fusion.23
  223.4 0.4 maximum_multiply_fusion
  223.9 0.4 fusion.29
  224.2 0.2 fusion.6
  224.4 0.3 fusion.5
  224.7 4.8 %convolution_convert_fusion = bf16[256,4096]{1,0:T(8,128)(2,1)} fusion(bf16[256,512]{0,1:T(8,128)(2,1)S(1)} %bitcast.73, bf16[4096,1280]{1,0:T(8,128)(2,1)} %all-gather.5.cloned.1.call-done), kind=kOutput, calls=%fused_computation.2 | convolution fusion | flops 1074790400 | bytes 6553600 | tf_op jit(solution)/shard_map/dot_general | solution.py:105
  229.6 0.7 pad_maximum_fusion.3
  230.3 85.7 %reduce-scatter.2.cloned.1.call-done = bf16[32,4096]{1,0:T(8,128)(2,1)} async-done(((bf16[256,4096]{1,0:T(8,128)(2,1)}), bf16[32,4096]{1,0:T(8,128)(2,1)}) %reduce-scatter.2.cloned.1.call-update) | async-done | bytes 262160 | tf_op jit(solution)/shard_map/reduce_scatter | solution.py:108
  316.0 1.7 fusion.11
  (19 shorter events, 0.7 us)
Async XLA Ops:
  7.2 78.1 %all-gather.3.cloned.1.call-start = ((), (), s32[]{:S(2)}) async-start(), calls=%async_computation.1 | async-start | bytes 2359296 | tf_op jit(solution)/shard_map/all_gather | solution.py:66
  10.8 206.5 %all-gather.5.cloned.1.call-start = ((), (), s32[]{:S(2)}) async-start(), calls=%async_computation.2 | async-start | bytes 10649600 | tf_op jit(solution)/shard_map/all_gather | solution.py:68
  12.5 303.4 %reduce-scatter.2.cloned.1.call-start = ((), (), s32[]{:S(2)}) async-start(), calls=%async_computation.3 | async-start | bytes 2359296 | tf_op jit(solution)/shard_map/reduce_scatter | solution.py:108
  224.7 91.2 %copy-start = (bf16[32,4096]{1,0:T(8,128)(2,1)S(1)}, bf16[32,4096]{1,0:T(8,128)(2,1)}, u32[]{:S(2)}) copy-start(bf16[32,4096]{1,0:T(8,128)(2,1)} %param.7) | copy-start | bytes 786436
Sparse Core Ops, SparseCore 0:
  11.8 73.4 all-gather.2
  87.4 129.8 all-gather.4
  229.7 86.1 reduce-scatter.1

commit v2 on v1

--- a/solution.py
+++ b/solution.py
@@ -63,7 +63,10 @@
     score_scale = HEAD ** (-0.5)
     rows_float = hidden_in.astype(jnp.float32)
     normed = rms_normed(rows_float, norm_gain)
-    gathered = lax.all_gather(normed, "tensor", axis=0, tiled=True)
+    tensor_size = pack_rows // normed.shape[0]
+    gathered = lax.all_to_all(
+        jnp.broadcast_to(normed[None], (tensor_size,) + normed.shape), "tensor", 0, 0, tiled=True
+    ).reshape(pack_rows, normed.shape[1])
     packed = jnp.concatenate((w_query, w_key, w_value, w_out.T), axis=1)
     packed_full = lax.all_gather(packed, "dp", axis=0, tiled=True)
     joined = packed_full[:, : query_cols + 2 * kv_cols]
@@ -105,12 +108,10 @@
     out_rows = lax.dot_general(
         attended, out_full_t, (((1,), (1,)), ((), ())), preferred_element_type=jnp.float32
     )
-    summed = lax.psum_scatter(
-        out_rows.astype(jnp.bfloat16),
-        "tensor",
-        scatter_dimension=0,
-        tiled=True,
-    ).astype(jnp.float32)
+    pieces = lax.all_to_all(
+        out_rows.astype(jnp.bfloat16).reshape(tensor_size, -1, out_rows.shape[1]), "tensor", 0, 0, tiled=True
+    )
+    summed = jnp.sum(pieces.astype(jnp.float32), axis=0)
     hidden_out = (summed + rows_float).astype(jnp.bfloat16)
     return (hidden_out, cache_rows)
 

time: 325 us -> 201 us (0.62)
  waiting for transfers between devices: 287 us -> 153 us
  starting transfers between devices: 0.12 us -> 13.3 us
  other arithmetic: 12.2 us -> 8.59 us
    reduce_scatter x1 -> x0, waiting for transfers between devices: 85.7 us -> none  [body(): lax.psum_scatter(out_rows.astype(jnp.bfloat16), 'tensor', scatter_dimensi...]
    all_gather x1 -> x0, waiting for transfers between devices: 69 us -> none  [body(): gathered = lax.all_gather(normed, 'tensor', axis=0, tiled=True)]
    all_to_all x0 -> x2, waiting for transfers between devices: none -> 58.5 us  [the longest x1 31.2 us: body(): lax.all_to_all(jnp.broadcast_to(normed[None], (tensor_size,) + normed.sha...]
    all_gather x1, waiting for transfers between devices: 132 us -> 94.2 us  [body(): packed_full = lax.all_gather(packed, 'dp', axis=0, tiled=True)]
    all_to_all x0 -> x2, starting transfers between devices: none -> 13.2 us  [the longest x1 7.47 us: body(): lax.all_to_all(jnp.broadcast_to(normed[None], (tensor_size,) + normed.sha...]
  transfers between devices with their start and end apart: 3 -> 3, of which waited for: 3 -> 3; matrix products, arithmetic and copies ran while one was open for 2% -> 3% of each run, Pallas kernels for 0% -> 0%
where the time goes in v2:
time: 201 us
  waiting for transfers between devices  153 us (76%)
  between operations  14.2 us (7%)
  starting transfers between devices  13.3 us (7%)
  matrix products  10 us (5%)
  other arithmetic  8.59 us (4%)
  local copies, waits for them, and re-layouts  2.09 us (1%)
    all_gather x1, waiting for transfers between devices, body(): packed_full = lax.all_gather(packed, 'dp', axis=0, tiled=True)  94.2 us
    all_to_all x1, waiting for transfers between devices, body(): lax.all_to_all(jnp.broadcast_to(normed[None], (tensor_size,) + normed.sha...  31.2 us
    all_to_all x1, waiting for transfers between devices, body(): lax.all_to_all(out_rows.astype(jnp.bfloat16).reshape(tensor_size, -1, out...  27.3 us
    all_to_all x1, starting transfers between devices, body(): lax.all_to_all(jnp.broadcast_to(normed[None], (tensor_size,) + normed.sha...  7.47 us
    all_to_all x1, starting transfers between devices, body(): lax.all_to_all(out_rows.astype(jnp.bfloat16).reshape(tensor_size, -1, out...  5.77 us
    dot_general x1, matrix products, body(): lax.dot_general(attended, out_full_t, (((1,), (1,)), ((), ())), preferred...  4.8 us
    dot_general x1, matrix products, body(): projected = jnp.dot(gathered, joined, preferred_element_type=jnp.float32)  4.56 us
  transfers between devices with their start and end apart: 3, of which 3 were waited for; matrix products, arithmetic and copies ran while one was open for 3% of the time, Pallas kernels for 0%

profile of v2, /device:TPU:1, one launch (start us, length us, event | category | flops | bytes accessed | tf_op | source)
XLA Modules:
  0.0 200.9 jit_solution(4414675054207526265)
XLA Ops:
  7.2 1.6 pad_maximum_fusion
  8.8 0.7 convert_element_type.62
  9.5 1.1 fusion.8
  10.7 1.1 fusion.10
  11.7 1.5 broadcast_in_dim.13
  13.3 7.5 %all-to-all-start = ((bf16[8,32,4096]{2,1,0:T(8,128)(2,1)}), bf16[8,32,4096]{2,1,0:T(8,128)(2,1)S(1)}, u32[]{:S(2)}, u32[]{:S(2)}) async-start(bf16[8,32,4096]{2,1,0:T(8,128)(2,1)} %broadcast_in_dim.13), calls=%async_computation | async-start | bytes 4194304 | tf_op jit(solution)/shard_map/all_to_all | solution.py:67
  20.9 0.3 reduce-window.9
  21.7 0.5 multiply_cosine_fusion
  22.2 31.2 %all-to-all-done = bf16[8,32,4096]{2,1,0:T(8,128)(2,1)S(1)} async-done(((bf16[8,32,4096]{2,1,0:T(8,128)(2,1)}), bf16[8,32,4096]{2,1,0:T(8,128)(2,1)S(1)}, u32[]{:S(2)}, u32[]{:S(2)}) %all-to-all-start) | async-done | bytes 2097184 | tf_op jit(solution)/shard_map/all_to_all | solution.py:67
  53.4 94.2 %all-gather.2.cloned.1.call-done = bf16[4096,1280]{1,0:T(8,128)(2,1)} async-done(((bf16[64,1280]{1,0:T(8,128)(2,1)}), bf16[4096,1280]{1,0:T(8,128)(2,1)}) %all-gather.2.cloned.1.call-update) | async-done | bytes 10485776 | tf_op jit(solution)/shard_map/all_gather | solution.py:71
  147.6 4.6 %fusion = f32[256,768]{1,0:T(8,128)S(1)} fusion(bf16[256,4096]{1,0:T(8,128)(2,1)S(1)} %bitcast.71, bf16[4096,1280]{1,0:T(8,128)(2,1)} %all-gather.2.cloned.1.call-done), kind=kOutput, calls=%fused_computation | convolution fusion | flops 1610612736 | bytes 9175040 | tf_op jit(solution)/shard_map/dot_general | solution.py:74
  152.4 0.2 reshape.137
  152.6 0.3 slice_negate_fusion
  152.9 0.2 fusion.23
  153.1 0.4 maximum_multiply_fusion
  153.6 0.4 fusion.29
  153.9 0.2 fusion.6
  154.1 0.3 fusion.5
  154.4 4.8 %convolution_convert_fusion = bf16[256,4096]{1,0:T(8,128)(2,1)} fusion(bf16[256,512]{0,1:T(8,128)(2,1)S(1)} %bitcast.77, bf16[4096,1280]{1,0:T(8,128)(2,1)} %all-gather.2.cloned.1.call-done), kind=kOutput, calls=%fused_computation.2 | convolution fusion | flops 1074790400 | bytes 6553600 | tf_op jit(solution)/shard_map/dot_general | solution.py:108
  159.2 5.8 %all-to-all-start.1 = ((bf16[8,32,4096]{2,1,0:T(8,128)(2,1)}), bf16[8,32,4096]{2,1,0:T(8,128)(2,1)S(1)}, u32[]{:S(2)}, u32[]{:S(2)}) async-start(bf16[8,32,4096]{2,1,0:T(8,128)(2,1)} %bitcast.72), calls=%async_computation.1 | async-start | bytes 4194304 | tf_op jit(solution)/shard_map/all_to_all | solution.py:111
  165.0 0.7 pad_maximum_fusion.3
  165.7 27.3 %all-to-all-done.1 = bf16[8,32,4096]{2,1,0:T(8,128)(2,1)S(1)} async-done(((bf16[8,32,4096]{2,1,0:T(8,128)(2,1)}), bf16[8,32,4096]{2,1,0:T(8,128)(2,1)S(1)}, u32[]{:S(2)}, u32[]{:S(2)}) %all-to-all-start.1) | async-done | bytes 2097184 | tf_op jit(solution)/shard_map/all_to_all | solution.py:111
  193.0 0.3 convert_reduce_fusion
  193.3 0.8 fusion.11
  (21 shorter events, 0.9 us)
Async XLA Ops:
  7.2 13.6 %copy-start.1 = (s32[256]{0:T(256)S(1)}, s32[256]{0:T(256)}, u32[]{:S(2)}) copy-start(s32[256]{0:T(256)} %param.13) | copy-start | bytes 3076
  7.2 140.5 %all-gather.2.cloned.1.call-start = ((), (), s32[]{:S(2)}) async-start(), calls=%async_computation.2 | async-start | bytes 10649600 | tf_op jit(solution)/shard_map/all_gather | solution.py:71
  13.3 40.1 %all-to-all-start = ((bf16[8,32,4096]{2,1,0:T(8,128)(2,1)}), bf16[8,32,4096]{2,1,0:T(8,128)(2,1)S(1)}, u32[]{:S(2)}, u32[]{:S(2)}) async-start(bf16[8,32,4096]{2,1,0:T(8,128)(2,1)} %broadcast_in_dim.13), calls=%async_computation | async-start | bytes 4194304 | tf_op jit(solution)/shard_map/all_to_all | solution.py:67
  159.2 34.0 %copy-start = (bf16[32,4096]{1,0:T(8,128)(2,1)S(1)}, bf16[32,4096]{1,0:T(8,128)(2,1)}, u32[]{:S(2)}) copy-start(bf16[32,4096]{1,0:T(8,128)(2,1)} %param.7) | copy-start | bytes 786436
  159.2 33.7 %all-to-all-start.1 = ((bf16[8,32,4096]{2,1,0:T(8,128)(2,1)}), bf16[8,32,4096]{2,1,0:T(8,128)(2,1)S(1)}, u32[]{:S(2)}, u32[]{:S(2)}) async-start(bf16[8,32,4096]{2,1,0:T(8,128)(2,1)} %bitcast.72), calls=%async_computation.1 | async-start | bytes 4194304 | tf_op jit(solution)/shard_map/all_to_all | solution.py:111
Sparse Core Ops, SparseCore 0:
  10.7 136.8 all-gather.1

commit v3 on v2

--- a/solution.py
+++ b/solution.py
@@ -1,7 +1,7 @@
 import jax
 import jax.numpy as jnp
 from jax import lax
-from jax.sharding import PartitionSpec as P
+from jax.sharding import Mesh, PartitionSpec as P
 
 HEAD = 128
 
@@ -61,14 +61,27 @@
     kv_heads = kv_cols // HEAD
     group_size = query_heads // kv_heads
     score_scale = HEAD ** (-0.5)
+    packed_rows = w_query.shape[0]
     rows_float = hidden_in.astype(jnp.float32)
     normed = rms_normed(rows_float, norm_gain)
     tensor_size = pack_rows // normed.shape[0]
+    first_core = lax.axis_index("c") == 0
+    split_d = normed.reshape(normed.shape[0], -1, 2, 2, packed_rows)
+    by_core = jnp.transpose(split_d, (0, 3, 1, 2, 4))
+    by_core = jnp.where(first_core, by_core, by_core[:, ::-1])
+    normed = by_core.reshape(normed.shape)
     gathered = lax.all_to_all(
         jnp.broadcast_to(normed[None], (tensor_size,) + normed.shape), "tensor", 0, 0, tiled=True
     ).reshape(pack_rows, normed.shape[1])
     packed = jnp.concatenate((w_query, w_key, w_value, w_out.T), axis=1)
-    packed_full = lax.all_gather(packed, "dp", axis=0, tiled=True)
+    pair = lax.ppermute(packed, "xl", [(0, 1), (1, 0)])
+    first_xl = lax.axis_index("xl") == 0
+    chip_pair = jnp.where(
+        first_xl, jnp.concatenate((packed, pair)), jnp.concatenate((pair, packed))
+    )
+    core_half = lax.all_gather(chip_pair, "z", axis=0, tiled=True)
+    other_half = lax.ppermute(core_half, "c", [(0, 1), (1, 0)])
+    packed_full = jnp.concatenate((core_half, other_half))
     joined = packed_full[:, : query_cols + 2 * kv_cols]
     out_full_t = packed_full[:, query_cols + 2 * kv_cols :]
     projected = jnp.dot(gathered, joined, preferred_element_type=jnp.float32)
@@ -112,23 +125,31 @@
         out_rows.astype(jnp.bfloat16).reshape(tensor_size, -1, out_rows.shape[1]), "tensor", 0, 0, tiled=True
     )
     summed = jnp.sum(pieces.astype(jnp.float32), axis=0)
+    split_s = summed.reshape(summed.shape[0], 2, -1, 2, packed_rows)
+    split_s = jnp.where(first_core, split_s, split_s[:, ::-1])
+    summed = jnp.transpose(split_s, (0, 2, 3, 1, 4)).reshape(summed.shape)
     hidden_out = (summed + rows_float).astype(jnp.bfloat16)
     return (hidden_out, cache_rows)
 
 
 def solution(mesh):
+    dp_size = mesh.shape["dp"]
+    chip_mesh = Mesh(
+        mesh.devices.reshape(dp_size // 4, 2, 2, mesh.shape["tensor"]), ("z", "xl", "c", "tensor")
+    )
+    dp = ("z", "xl", "c")
     return jax.shard_map(
         body,
-        mesh=mesh,
+        mesh=chip_mesh,
         in_specs=(
-            P(("dp", "tensor"), None),
+            P((*dp, "tensor"), None),
             P(),
-            P("dp", "tensor"),
-            P("dp", "tensor"),
-            P("dp", "tensor"),
-            P("tensor", "dp"),
-            P("dp"),
+            P(dp, "tensor"),
+            P(dp, "tensor"),
+            P(dp, "tensor"),
+            P("tensor", dp),
+            P(dp),
         ),
-        out_specs=(P(("dp", "tensor"), None), P("dp", "tensor", None)),
+        out_specs=(P((*dp, "tensor"), None), P(dp, "tensor", None)),
         check_vma=False,
     )

time: 201 us -> 208 us (1.035)
  waiting for transfers between devices: 153 us -> 125 us
  local copies, waits for them, and re-layouts: 2.09 us -> 21.9 us
  starting transfers between devices: 13.3 us -> 24.3 us
  other arithmetic: 8.59 us -> 11.4 us
    all_to_all x1, waiting for transfers between devices: 31.2 us -> 16.5 us  [body(): lax.all_to_all(jnp.broadcast_to(normed[None], (tensor_size,) + normed.sha...]
    all_gather x1, waiting for transfers between devices: 94.2 us -> 79.7 us  [body(): core_half = lax.all_gather(chip_pair, 'z', axis=0, tiled=True)]
    ppermute x0 -> x2, starting transfers between devices: none -> 14 us  [the longest x1 10.1 us: body(): other_half = lax.ppermute(core_half, 'c', [(0, 1), (1, 0)])]
    rev x0 -> x2, local copies, waits for them, and re-layouts: none -> 5.53 us  [the longest x1 2.78 us: body(): split_s = jnp.where(first_core, split_s, split_s[:, ::-1])]
    concatenate x0 -> x1, local copies, waits for them, and re-layouts: none -> 5.17 us  [body(): packed_full = jnp.concatenate((core_half, other_half))]
    unnamed x4 -> x5, local copies, waits for them, and re-layouts: 0.01 us -> 5.15 us
    reshape x0 -> x4, local copies, waits for them, and re-layouts: none -> 3.08 us  [the longest x2 1.6 us: body(): split_s = summed.reshape(summed.shape[0], 2, -1, 2, packed_rows)]
    ppermute x0 -> x2, waiting for transfers between devices: none -> 2.69 us  [the longest x1 2.69 us: body(): pair = lax.ppermute(packed, 'xl', [(0, 1), (1, 0)])]
  transfers between devices with their start and end apart: 3 -> 5, of which waited for: 3 -> 4; matrix products, arithmetic and copies ran while one was open for 3% -> 10% of each run, Pallas kernels for 0% -> 0%
where the time goes in v3:
time: 208 us; the launch traced here: 207 us
  waiting for transfers between devices  125 us (60%)
  starting transfers between devices  24.3 us (12%)
  local copies, waits for them, and re-layouts  21.9 us (11%)
  between operations  14.3 us (7%)
  other arithmetic  11.4 us (5%)
  matrix products  10 us (5%)
    all_gather x1, waiting for transfers between devices, body(): core_half = lax.all_gather(chip_pair, 'z', axis=0, tiled=True)  79.7 us
    all_to_all x1, waiting for transfers between devices, body(): lax.all_to_all(out_rows.astype(jnp.bfloat16).reshape(tensor_size, -1, out...  26.4 us
    all_to_all x1, waiting for transfers between devices, body(): lax.all_to_all(jnp.broadcast_to(normed[None], (tensor_size,) + normed.sha...  16.5 us
    ppermute x1, starting transfers between devices, body(): other_half = lax.ppermute(core_half, 'c', [(0, 1), (1, 0)])  10.1 us
    all_to_all x1, starting transfers between devices, body(): lax.all_to_all(jnp.broadcast_to(normed[None], (tensor_size,) + normed.sha...  6.42 us
    concatenate x1, local copies, waits for them, and re-layouts, body(): packed_full = jnp.concatenate((core_half, other_half))  5.17 us
    unnamed x5, local copies, waits for them, and re-layouts  5.15 us
    dot_general x1, matrix products, body(): lax.dot_general(attended, out_full_t, (((1,), (1,)), ((), ())), preferred...  4.8 us
  transfers between devices with their start and end apart: 5, of which 4 were waited for; matrix products, arithmetic and copies ran while one was open for 10% of the time, Pallas kernels for 0%

profile of v3, /device:TPU:1, one launch (start us, length us, event | category | flops | bytes accessed | tf_op | source)
XLA Modules:
  0.0 207.1 jit_solution(18170428994764543220)
XLA Ops:
  7.2 0.9 pad_maximum_fusion
  8.1 3.9 %collective-permute-start = (bf16[64,1280]{1,0:T(8,128)(2,1)S(1)}, bf16[64,1280]{1,0:T(8,128)(2,1)S(1)}, u32[]{:S(2)}, u32[]{:S(2)}) collective-permute-start(bf16[64,1280]{1,0:T(8,128)(2,1)S(1)} %pad_maximum_fusion), channel_id=1, source_target_pairs={{0,16},{16,0},{1,17},{17,1},{2,18},{18,2},{3,19},{19,3},{4,20},{20... | collective-permute-start | bytes 491528 | tf_op jit(solution)/shard_map/ppermute | solution.py:77
  12.1 2.7 %collective-permute-done = bf16[64,1280]{1,0:T(8,128)(2,1)S(1)} collective-permute-done((bf16[64,1280]{1,0:T(8,128)(2,1)S(1)}, bf16[64,1280]{1,0:T(8,128)(2,1)S(1)}, u32[]{:S(2)}, u32[]{:S(2)}) %collective-permute-start) | collective-permute-done | bytes 163872 | tf_op jit(solution)/shard_map/ppermute | solution.py:77
  14.8 1.8 maximum_select_fusion
  16.6 79.7 %all-gather.2.cloned.1.call-done = bf16[2048,1280]{1,0:T(8,128)(2,1)} async-done(((bf16[128,1280]{1,0:T(8,128)(2,1)}), bf16[2048,1280]{1,0:T(8,128)(2,1)}) %all-gather.2.cloned.1.call-update) | async-done | bytes 5242896 | tf_op jit(solution)/shard_map/all_gather | solution.py:82
  96.3 10.1 %collective-permute-start.1 = (bf16[2048,1280]{1,0:T(8,128)(2,1)}, bf16[2048,1280]{1,0:T(8,128)(2,1)}, u32[]{:S(2)}, u32[]{:S(2)}) collective-permute-start(bf16[2048,1280]{1,0:T(8,128)(2,1)} %all-gather.2.cloned.1.call-done), channel_id=1, source_target_pairs={{0,8},{8,0},{1,9},{9,1},{2,10},{10,2},{3,11},{11,3},{4,12},{12,4},... | collective-permute-start | bytes 15728648 | tf_op jit(solution)/shard_map/ppermute | solution.py:83
  107.1 1.1 fusion.8
  108.2 1.1 fusion.10
  109.8 2.7 %rev.6 = bf16[32,2,16,2,64]{4,1,3,2,0:T(2,128)(2,1)S(1)} reverse(bf16[32,2,16,2,64]{4,1,3,2,0:T(2,128)(2,1)S(1)} %bitcast.75), dimensions={1} | reverse | bytes 524288 | tf_op jit(solution)/shard_map/rev | solution.py:71
  114.0 1.6 broadcast_in_dim.16
  115.6 6.4 %all-to-all-start = ((bf16[8,32,4096]{2,1,0:T(8,128)(2,1)}), bf16[8,32,4096]{2,1,0:T(8,128)(2,1)S(1)}, u32[]{:S(2)}, u32[]{:S(2)}) async-start(bf16[8,32,4096]{2,1,0:T(8,128)(2,1)} %broadcast_in_dim.16), calls=%async_computation | async-start | bytes 4194304 | tf_op jit(solution)/shard_map/all_to_all | solution.py:73
  123.5 5.1 %constant_dynamic-update-slice_fusion.1 = bf16[4096,1280]{1,0:T(8,128)(2,1)} fusion(bf16[2048,1280]{1,0:T(8,128)(2,1)} %all-gather.2.cloned.1.call-done), kind=kLoop, calls=%fused_computation.55 | loop fusion | bytes 10485760
  128.6 5.2 %constant_dynamic-update-slice_fusion = bf16[4096,1280]{1,0:T(8,128)(2,1)} fusion(bf16[4096,1280]{1,0:T(8,128)(2,1)} %constant_dynamic-update-slice_fusion.1, bf16[2048,1280]{1,0:T(8,128)(2,1)} %collective-permute-done.1), kind=kLoop, calls=%fused_computation.54 | loop fusion | bytes 10485760 | tf_op jit(solution)/shard_map/concatenate | solution.py:84
  133.8 16.5 %all-to-all-done = bf16[8,32,4096]{2,1,0:T(8,128)(2,1)S(1)} async-done(((bf16[8,32,4096]{2,1,0:T(8,128)(2,1)}), bf16[8,32,4096]{2,1,0:T(8,128)(2,1)S(1)}, u32[]{:S(2)}, u32[]{:S(2)}) %all-to-all-start) | async-done | bytes 2097184 | tf_op jit(solution)/shard_map/all_to_all | solution.py:73
  150.2 4.6 %fusion = f32[256,768]{1,0:T(8,128)S(1)} fusion(bf16[256,4096]{1,0:T(8,128)(2,1)S(1)} %bitcast.76, bf16[4096,1280]{1,0:T(8,128)(2,1)} %constant_dynamic-update-slice_fusion), kind=kOutput, calls=%fused_computation | convolution fusion | flops 1610612736 | bytes 9175040 | tf_op jit(solution)/shard_map/dot_general | solution.py:87
  157.0 4.8 %convolution_convert_fusion = bf16[256,4096]{1,0:T(8,128)(2,1)} fusion(bf16[256,512]{0,1:T(8,128)(2,1)S(1)} %bitcast.83, bf16[4096,1280]{1,0:T(8,128)(2,1)} %constant_dynamic-update-slice_fusion), kind=kOutput, calls=%fused_computation.2 | convolution fusion | flops 1074790400 | bytes 6553600 | tf_op jit(solution)/shard_map/dot_general | solution.py:121
  161.8 3.8 %all-to-all-start.1 = ((bf16[8,32,4096]{2,1,0:T(8,128)(2,1)}), bf16[8,32,4096]{2,1,0:T(8,128)(2,1)S(1)}, u32[]{:S(2)}, u32[]{:S(2)}) async-start(bf16[8,32,4096]{2,1,0:T(8,128)(2,1)} %bitcast.77), calls=%async_computation.1 | async-start | bytes 4194304 | tf_op jit(solution)/shard_map/all_to_all | solution.py:124
  166.3 26.4 %all-to-all-done.1 = bf16[8,32,4096]{2,1,0:T(8,128)(2,1)S(1)} async-done(((bf16[8,32,4096]{2,1,0:T(8,128)(2,1)}), bf16[8,32,4096]{2,1,0:T(8,128)(2,1)S(1)}, u32[]{:S(2)}, u32[]{:S(2)}) %all-to-all-start.1) | async-done | bytes 2097184 | tf_op jit(solution)/shard_map/all_to_all | solution.py:124
  193.0 0.8 reshape.151
  193.8 0.8 copy.20
  194.6 2.8 %rev.7 = f32[32,2,16,2,64]{4,1,3,2,0:T(2,128)S(1)} reverse(f32[32,2,16,2,64]{4,1,3,2,0:T(2,128)S(1)} %copy.20), dimensions={1} | reverse | bytes 1048576 | tf_op jit(solution)/shard_map/rev | solution.py:129
  197.4 1.1 select_bitcast_fusion
  198.5 0.9 reshape.152
  199.5 0.8 fusion.11
  (38 shorter events, 7.3 us)
Async XLA Ops:
  7.2 89.1 %all-gather.2.cloned.1.call-start = ((), (), s32[]{:S(2)}) async-start(), calls=%async_computation.2 | async-start | bytes 5570560 | tf_op jit(solution)/shard_map/all_gather | solution.py:82
  8.1 6.6 %collective-permute-start = (bf16[64,1280]{1,0:T(8,128)(2,1)S(1)}, bf16[64,1280]{1,0:T(8,128)(2,1)S(1)}, u32[]{:S(2)}, u32[]{:S(2)}) collective-permute-start(bf16[64,1280]{1,0:T(8,128)(2,1)S(1)} %pad_maximum_fusion), channel_id=1, source_target_pairs={{0,16},{16,0},{1,17},{17,1},{2,18},{18,2},{3,19},{19,3},{4,20},{20... | collective-permute-start | bytes 491528 | tf_op jit(solution)/shard_map/ppermute | solution.py:77
  96.3 32.3 %collective-permute-start.1 = (bf16[2048,1280]{1,0:T(8,128)(2,1)}, bf16[2048,1280]{1,0:T(8,128)(2,1)}, u32[]{:S(2)}, u32[]{:S(2)}) collective-permute-start(bf16[2048,1280]{1,0:T(8,128)(2,1)} %all-gather.2.cloned.1.call-done), channel_id=1, source_target_pairs={{0,8},{8,0},{1,9},{9,1},{2,10},{10,2},{3,11},{11,3},{4,12},{12,4},... | collective-permute-start | bytes 15728648 | tf_op jit(solution)/shard_map/ppermute | solution.py:83
  112.6 9.4 %copy-start.1 = (s32[256]{0:T(256)S(1)}, s32[256]{0:T(256)}, u32[]{:S(2)}) copy-start(s32[256]{0:T(256)} %param.13) | copy-start | bytes 3076
  115.6 34.7 %all-to-all-start = ((bf16[8,32,4096]{2,1,0:T(8,128)(2,1)}), bf16[8,32,4096]{2,1,0:T(8,128)(2,1)S(1)}, u32[]{:S(2)}, u32[]{:S(2)}) async-start(bf16[8,32,4096]{2,1,0:T(8,128)(2,1)} %broadcast_in_dim.16), calls=%async_computation | async-start | bytes 4194304 | tf_op jit(solution)/shard_map/all_to_all | solution.py:73
  161.8 30.9 %all-to-all-start.1 = ((bf16[8,32,4096]{2,1,0:T(8,128)(2,1)}), bf16[8,32,4096]{2,1,0:T(8,128)(2,1)S(1)}, u32[]{:S(2)}, u32[]{:S(2)}) async-start(bf16[8,32,4096]{2,1,0:T(8,128)(2,1)} %bitcast.77), calls=%async_computation.1 | async-start | bytes 4194304 | tf_op jit(solution)/shard_map/all_to_all | solution.py:124
  193.0 6.5 %copy-start = (bf16[32,4096]{1,0:T(8,128)(2,1)S(1)}, bf16[32,4096]{1,0:T(8,128)(2,1)}, u32[]{:S(2)}) copy-start(bf16[32,4096]{1,0:T(8,128)(2,1)} %param.7) | copy-start | bytes 786436
Sparse Core Ops, SparseCore 0:
  16.7 79.5 all-gather.1

commit v4 on v3

--- a/solution.py
+++ b/solution.py
@@ -53,7 +53,7 @@
     return same_segment & causal | (key_index[None, :] == row_index[:, None])
 
 
-def body(hidden_in, norm_gain, w_query, w_key, w_value, w_out, segment):
+def layer(hidden_in, norm_gain, w_query, w_key, w_value, w_out, segment):
     pack_rows = segment.shape[0]
     query_cols = w_query.shape[1]
     kv_cols = w_key.shape[1]
@@ -81,10 +81,13 @@
     )
     core_half = lax.all_gather(chip_pair, "z", axis=0, tiled=True)
     other_half = lax.ppermute(core_half, "c", [(0, 1), (1, 0)])
-    packed_full = jnp.concatenate((core_half, other_half))
-    joined = packed_full[:, : query_cols + 2 * kv_cols]
-    out_full_t = packed_full[:, query_cols + 2 * kv_cols :]
-    projected = jnp.dot(gathered, joined, preferred_element_type=jnp.float32)
+    half_rows = core_half.shape[0]
+    proj_cols = query_cols + 2 * kv_cols
+    projected = jnp.dot(
+        gathered[:, :half_rows], core_half[:, :proj_cols], preferred_element_type=jnp.float32
+    ) + jnp.dot(
+        gathered[:, half_rows:], other_half[:, :proj_cols], preferred_element_type=jnp.float32
+    )
     position = positions_of(segment)
     query_rows = rotate(
         projected[:, :query_cols].reshape(pack_rows, query_heads, HEAD), position
@@ -118,8 +121,13 @@
     attended = (
         jnp.transpose(mixed_rows, (2, 0, 1, 3)).astype(jnp.bfloat16).reshape(pack_rows, query_cols)
     )
-    out_rows = lax.dot_general(
-        attended, out_full_t, (((1,), (1,)), ((), ())), preferred_element_type=jnp.float32
+    out_dims = (((1,), (1,)), ((), ()))
+    out_rows = jnp.concatenate(
+        (
+            lax.dot_general(attended, core_half[:, proj_cols:], out_dims, preferred_element_type=jnp.float32),
+            lax.dot_general(attended, other_half[:, proj_cols:], out_dims, preferred_element_type=jnp.float32),
+        ),
+        axis=1,
     )
     pieces = lax.all_to_all(
         out_rows.astype(jnp.bfloat16).reshape(tensor_size, -1, out_rows.shape[1]), "tensor", 0, 0, tiled=True
@@ -139,7 +147,7 @@
     )
     dp = ("z", "xl", "c")
     return jax.shard_map(
-        body,
+        layer,
         mesh=chip_mesh,
         in_specs=(
             P((*dp, "tensor"), None),

time: 208 us -> 211 us (1.014)
  waiting for transfers between devices: 125 us -> 136 us
  local copies, waits for them, and re-layouts: 21.9 us -> 11.9 us
    all_to_all x2, waiting for transfers between devices: 42.9 us -> 53.2 us  [the longest x1 26.8 us: layer(): lax.all_to_all(jnp.broadcast_to(normed[None], (tensor_size,) + normed.sha...]
    concatenate x1 -> x0, local copies, waits for them, and re-layouts: 5.17 us -> none  [body(): packed_full = jnp.concatenate((core_half, other_half))]
    unnamed x5 -> x4, local copies, waits for them, and re-layouts: 5.15 us -> 0.01 us
    dot_general x4 -> x6, matrix products: 10 us -> 11.1 us  [the longest x1 2.87 us: layer(): jnp.dot(gathered[:, :half_rows], core_half[:, :proj_cols], preferred_elem...]
  transfers between devices with their start and end apart: 5 -> 5, of which waited for: 4 -> 4; matrix products, arithmetic and copies ran while one was open for 10% -> 5% of each run, Pallas kernels for 0% -> 0%
where the time goes in v4:
time: 211 us; the launch traced here: 210 us
  waiting for transfers between devices  136 us (64%)
  starting transfers between devices  24.3 us (12%)
  between operations  14.3 us (7%)
  other arithmetic  12.9 us (6%)
  local copies, waits for them, and re-layouts  11.9 us (6%)
  matrix products  11.1 us (5%)
    all_gather x1, waiting for transfers between devices, layer(): core_half = lax.all_gather(chip_pair, 'z', axis=0, tiled=True)  79.7 us
    all_to_all x1, waiting for transfers between devices, layer(): lax.all_to_all(jnp.broadcast_to(normed[None], (tensor_size,) + normed.sha...  26.8 us
    all_to_all x1, waiting for transfers between devices, layer(): lax.all_to_all(out_rows.astype(jnp.bfloat16).reshape(tensor_size, -1, out...  26.4 us
    ppermute x1, starting transfers between devices, layer(): other_half = lax.ppermute(core_half, 'c', [(0, 1), (1, 0)])  10.1 us
    all_to_all x1, starting transfers between devices, layer(): lax.all_to_all(jnp.broadcast_to(normed[None], (tensor_size,) + normed.sha...  6.42 us
  transfers between devices with their start and end apart: 5, of which 4 were waited for; matrix products, arithmetic and copies ran while one was open for 5% of the time, Pallas kernels for 0%

profile of v4, /device:TPU:1, one launch (start us, length us, event | category | flops | bytes accessed | tf_op | source)
XLA Modules:
  0.0 210.1 jit_solution(3950452128050506153)
XLA Ops:
  7.2 0.9 pad_maximum_fusion.1
  8.1 3.9 %collective-permute-start = (bf16[64,1280]{1,0:T(8,128)(2,1)S(1)}, bf16[64,1280]{1,0:T(8,128)(2,1)S(1)}, u32[]{:S(2)}, u32[]{:S(2)}) collective-permute-start(bf16[64,1280]{1,0:T(8,128)(2,1)S(1)} %pad_maximum_fusion.1), channel_id=1, source_target_pairs={{0,16},{16,0},{1,17},{17,1},{2,18},{18,2},{3,19},{19,3},{4,20},{20... | collective-permute-start | bytes 491528 | tf_op jit(solution)/shard_map/ppermute | solution.py:77
  12.1 2.7 %collective-permute-done = bf16[64,1280]{1,0:T(8,128)(2,1)S(1)} collective-permute-done((bf16[64,1280]{1,0:T(8,128)(2,1)S(1)}, bf16[64,1280]{1,0:T(8,128)(2,1)S(1)}, u32[]{:S(2)}, u32[]{:S(2)}) %collective-permute-start) | collective-permute-done | bytes 163872 | tf_op jit(solution)/shard_map/ppermute | solution.py:77
  14.8 1.8 maximum_select_fusion
  16.6 79.7 %all-gather.2.cloned.1.call-done = bf16[2048,1280]{1,0:T(8,128)(2,1)} async-done(((bf16[128,1280]{1,0:T(8,128)(2,1)}), bf16[2048,1280]{1,0:T(8,128)(2,1)}) %all-gather.2.cloned.1.call-update) | async-done | bytes 5242896 | tf_op jit(solution)/shard_map/all_gather | solution.py:82
  96.3 10.1 %collective-permute-start.1 = (bf16[2048,1280]{1,0:T(8,128)(2,1)}, bf16[2048,1280]{1,0:T(8,128)(2,1)}, u32[]{:S(2)}, u32[]{:S(2)}) collective-permute-start(bf16[2048,1280]{1,0:T(8,128)(2,1)} %all-gather.2.cloned.1.call-done), channel_id=1, source_target_pairs={{0,8},{8,0},{1,9},{9,1},{2,10},{10,2},{3,11},{11,3},{4,12},{12,4},... | collective-permute-start | bytes 15728648 | tf_op jit(solution)/shard_map/ppermute | solution.py:83
  107.1 1.1 fusion.15
  108.2 1.1 fusion.17
  109.9 2.7 %rev.6 = bf16[32,2,16,2,64]{4,1,3,2,0:T(2,128)(2,1)S(1)} reverse(bf16[32,2,16,2,64]{4,1,3,2,0:T(2,128)(2,1)S(1)} %bitcast.81), dimensions={1} | reverse | bytes 524288 | tf_op jit(solution)/shard_map/rev | solution.py:71
  114.0 1.5 broadcast_in_dim.16
  115.6 6.4 %all-to-all-start = ((bf16[8,32,4096]{2,1,0:T(8,128)(2,1)}), bf16[8,32,4096]{2,1,0:T(8,128)(2,1)S(1)}, u32[]{:S(2)}, u32[]{:S(2)}) async-start(bf16[8,32,4096]{2,1,0:T(8,128)(2,1)} %broadcast_in_dim.16), calls=%async_computation | async-start | bytes 4194304 | tf_op jit(solution)/shard_map/all_to_all | solution.py:73
  123.4 26.8 %all-to-all-done = bf16[8,32,4096]{2,1,0:T(8,128)(2,1)S(1)} async-done(((bf16[8,32,4096]{2,1,0:T(8,128)(2,1)}), bf16[8,32,4096]{2,1,0:T(8,128)(2,1)S(1)}, u32[]{:S(2)}, u32[]{:S(2)}) %all-to-all-start) | async-done | bytes 2097184 | tf_op jit(solution)/shard_map/all_to_all | solution.py:73
  150.2 2.9 %fusion = f32[256,768]{1,0:T(8,128)S(1)} fusion(bf16[2048,1280]{1,0:T(8,128)(2,1)} %collective-permute-done.1, bf16[256,4096]{1,0:T(8,128)(2,1)S(1)} %bitcast.82), kind=kOutput, calls=%fused_computation.1 | convolution fusion | flops 805306368 | bytes 4980736 | tf_op jit(solution)/shard_map/dot_general | solution.py:88
  153.1 2.9 %fusion.5 = f32[256,768]{1,0:T(8,128)S(1)} fusion(f32[256,768]{1,0:T(8,128)S(1)} %fusion, bf16[2048,1280]{1,0:T(8,128)(2,1)} %all-gather.2.cloned.1.call-done, bf16[256,4096]{1,0:T(8,128)(2,1)S(1)} %bitcast.83), kind=kOutput, calls=%fused_computation.12 | convolution fusion | flops 805502976 | bytes 5767168 | tf_op jit(solution)/shard_map/dot_general | solution.py:86
  158.6 2.3 %convolution_convert_fusion = bf16[8,32,2048]{2,1,0:T(8,128)(2,1)S(1)} fusion(bf16[8,32,512]{2,1,0:T(8,128)(2,1)S(1)} %dot_general.24, bf16[2048,1280]{1,0:T(8,128)(2,1)} %collective-permute-done.1), kind=kOutput, calls=%fused_computation.5 | convolution fusion | flops 537395200 | bytes 3407872 | tf_op jit(solution)/shard_map/dot_general | solution.py:128
  160.9 2.3 %convolution_convert_fusion.1 = bf16[8,32,2048]{2,1,0:T(8,128)(2,1)S(1)} fusion(bf16[8,32,512]{2,1,0:T(8,128)(2,1)S(1)} %dot_general.24, bf16[2048,1280]{1,0:T(8,128)(2,1)} %all-gather.2.cloned.1.call-done), kind=kOutput, calls=%fused_computation.6 | convolution fusion | flops 537395200 | bytes 3407872 | tf_op jit(solution)/shard_map/dot_general | solution.py:127
  163.2 1.6 pad_maximum_fusion
  164.8 3.8 %all-to-all-start.1 = ((bf16[8,32,4096]{2,1,0:T(8,128)(2,1)}), bf16[8,32,4096]{2,1,0:T(8,128)(2,1)S(1)}, u32[]{:S(2)}, u32[]{:S(2)}) async-start(bf16[8,32,4096]{2,1,0:T(8,128)(2,1)} %pad_maximum_fusion), calls=%async_computation.1 | async-start | bytes 4194304 | tf_op jit(solution)/shard_map/all_to_all | solution.py:132
  169.3 26.4 %all-to-all-done.1 = bf16[8,32,4096]{2,1,0:T(8,128)(2,1)S(1)} async-done(((bf16[8,32,4096]{2,1,0:T(8,128)(2,1)}), bf16[8,32,4096]{2,1,0:T(8,128)(2,1)S(1)}, u32[]{:S(2)}, u32[]{:S(2)}) %all-to-all-start.1) | async-done | bytes 2097184 | tf_op jit(solution)/shard_map/all_to_all | solution.py:132
  196.0 0.8 reshape.151
  196.8 0.8 copy.19
  197.6 2.8 %rev.7 = f32[32,2,16,2,64]{4,1,3,2,0:T(2,128)S(1)} reverse(f32[32,2,16,2,64]{4,1,3,2,0:T(2,128)S(1)} %copy.19), dimensions={1} | reverse | bytes 1048576 | tf_op jit(solution)/shard_map/rev | solution.py:137
  200.4 1.1 select_bitcast_fusion
  201.5 0.9 reshape.152
  (41 shorter events, 8.4 us)
Async XLA Ops:
  7.2 89.1 %all-gather.2.cloned.1.call-start = ((), (), s32[]{:S(2)}) async-start(), calls=%async_computation.2 | async-start | bytes 5570560 | tf_op jit(solution)/shard_map/all_gather | solution.py:82
  8.1 6.6 %collective-permute-start = (bf16[64,1280]{1,0:T(8,128)(2,1)S(1)}, bf16[64,1280]{1,0:T(8,128)(2,1)S(1)}, u32[]{:S(2)}, u32[]{:S(2)}) collective-permute-start(bf16[64,1280]{1,0:T(8,128)(2,1)S(1)} %pad_maximum_fusion.1), channel_id=1, source_target_pairs={{0,16},{16,0},{1,17},{17,1},{2,18},{18,2},{3,19},{19,3},{4,20},{20... | collective-permute-start | bytes 491528 | tf_op jit(solution)/shard_map/ppermute | solution.py:77
  96.3 53.9 %collective-permute-start.1 = (bf16[2048,1280]{1,0:T(8,128)(2,1)}, bf16[2048,1280]{1,0:T(8,128)(2,1)}, u32[]{:S(2)}, u32[]{:S(2)}) collective-permute-start(bf16[2048,1280]{1,0:T(8,128)(2,1)} %all-gather.2.cloned.1.call-done), channel_id=1, source_target_pairs={{0,8},{8,0},{1,9},{9,1},{2,10},{10,2},{3,11},{11,3},{4,12},{12,4},... | collective-permute-start | bytes 15728648 | tf_op jit(solution)/shard_map/ppermute | solution.py:83
  114.0 8.0 %copy-start.1 = (s32[256]{0:T(256)S(1)}, s32[256]{0:T(256)}, u32[]{:S(2)}) copy-start(s32[256]{0:T(256)} %param.13) | copy-start | bytes 3076
  115.6 34.7 %all-to-all-start = ((bf16[8,32,4096]{2,1,0:T(8,128)(2,1)}), bf16[8,32,4096]{2,1,0:T(8,128)(2,1)S(1)}, u32[]{:S(2)}, u32[]{:S(2)}) async-start(bf16[8,32,4096]{2,1,0:T(8,128)(2,1)} %broadcast_in_dim.16), calls=%async_computation | async-start | bytes 4194304 | tf_op jit(solution)/shard_map/all_to_all | solution.py:73
  164.8 30.9 %all-to-all-start.1 = ((bf16[8,32,4096]{2,1,0:T(8,128)(2,1)}), bf16[8,32,4096]{2,1,0:T(8,128)(2,1)S(1)}, u32[]{:S(2)}, u32[]{:S(2)}) async-start(bf16[8,32,4096]{2,1,0:T(8,128)(2,1)} %pad_maximum_fusion), calls=%async_computation.1 | async-start | bytes 4194304 | tf_op jit(solution)/shard_map/all_to_all | solution.py:132
  197.6 4.9 %copy-start = (bf16[32,4096]{1,0:T(8,128)(2,1)S(1)}, bf16[32,4096]{1,0:T(8,128)(2,1)}, u32[]{:S(2)}) copy-start(bf16[32,4096]{1,0:T(8,128)(2,1)} %param.7) | copy-start | bytes 786436
Sparse Core Ops, SparseCore 0:
  16.7 79.5 all-gather.1

commit v5 on v4

--- a/solution.py
+++ b/solution.py
@@ -65,10 +65,10 @@
     rows_float = hidden_in.astype(jnp.float32)
     normed = rms_normed(rows_float, norm_gain)
     tensor_size = pack_rows // normed.shape[0]
-    first_core = lax.axis_index("c") == 0
+    core = lax.axis_index("c")
     split_d = normed.reshape(normed.shape[0], -1, 2, 2, packed_rows)
-    by_core = jnp.transpose(split_d, (0, 3, 1, 2, 4))
-    by_core = jnp.where(first_core, by_core, by_core[:, ::-1])
+    by_core = jnp.transpose(split_d, (0, 3, 1, 2, 4)).reshape(normed.shape[0], 2, -1)
+    by_core = lax.dynamic_slice_in_dim(jnp.concatenate((by_core, by_core), axis=1), core, 2, axis=1)
     normed = by_core.reshape(normed.shape)
     gathered = lax.all_to_all(
         jnp.broadcast_to(normed[None], (tensor_size,) + normed.shape), "tensor", 0, 0, tiled=True
@@ -133,8 +133,9 @@
         out_rows.astype(jnp.bfloat16).reshape(tensor_size, -1, out_rows.shape[1]), "tensor", 0, 0, tiled=True
     )
     summed = jnp.sum(pieces.astype(jnp.float32), axis=0)
-    split_s = summed.reshape(summed.shape[0], 2, -1, 2, packed_rows)
-    split_s = jnp.where(first_core, split_s, split_s[:, ::-1])
+    split_s = summed.reshape(summed.shape[0], 2, -1)
+    split_s = lax.dynamic_slice_in_dim(jnp.concatenate((split_s, split_s), axis=1), core, 2, axis=1)
+    split_s = split_s.reshape(summed.shape[0], 2, -1, 2, packed_rows)
     summed = jnp.transpose(split_s, (0, 2, 3, 1, 4)).reshape(summed.shape)
     hidden_out = (summed + rows_float).astype(jnp.bfloat16)
     return (hidden_out, cache_rows)

time: 211 us -> 205 us (0.972)
  local copies, waits for them, and re-layouts: 11.9 us -> 7.01 us
    rev x2 -> x0, local copies, waits for them, and re-layouts: 5.53 us -> none  [the longest x1 2.78 us: layer(): split_s = jnp.where(first_core, split_s, split_s[:, ::-1])]
  transfers between devices with their start and end apart: 5 -> 5, of which waited for: 4 -> 4; matrix products, arithmetic and copies ran while one was open for 5% -> 4% of each run, Pallas kernels for 0% -> 0%
where the time goes in v5:
time: 205 us; the launch traced here: 204 us
  waiting for transfers between devices  136 us (66%)
  starting transfers between devices  24.3 us (12%)
  between operations  14.3 us (7%)
  other arithmetic  12.2 us (6%)
  matrix products  11.1 us (5%)
  local copies, waits for them, and re-layouts  7.01 us (3%)
    all_gather x1, waiting for transfers between devices, layer(): core_half = lax.all_gather(chip_pair, 'z', axis=0, tiled=True)  79.7 us
    all_to_all x1, waiting for transfers between devices, layer(): lax.all_to_all(jnp.broadcast_to(normed[None], (tensor_size,) + normed.sha...  26.8 us
    all_to_all x1, waiting for transfers between devices, layer(): lax.all_to_all(out_rows.astype(jnp.bfloat16).reshape(tensor_size, -1, out...  26.4 us
    ppermute x1, starting transfers between devices, layer(): other_half = lax.ppermute(core_half, 'c', [(0, 1), (1, 0)])  10.1 us
    all_to_all x1, starting transfers between devices, layer(): lax.all_to_all(jnp.broadcast_to(normed[None], (tensor_size,) + normed.sha...  6.42 us
  transfers between devices with their start and end apart: 5, of which 4 were waited for; matrix products, arithmetic and copies ran while one was open for 4% of the time, Pallas kernels for 0%

profile of v5, /device:TPU:1, one launch (start us, length us, event | category | flops | bytes accessed | tf_op | source)
XLA Modules:
  0.0 204.5 jit_solution(12138097571478553314)
XLA Ops:
  7.2 0.9 pad_maximum_fusion.1
  8.1 3.9 %collective-permute-start = (bf16[64,1280]{1,0:T(8,128)(2,1)S(1)}, bf16[64,1280]{1,0:T(8,128)(2,1)S(1)}, u32[]{:S(2)}, u32[]{:S(2)}) collective-permute-start(bf16[64,1280]{1,0:T(8,128)(2,1)S(1)} %pad_maximum_fusion.1), channel_id=1, source_target_pairs={{0,16},{16,0},{1,17},{17,1},{2,18},{18,2},{3,19},{19,3},{4,20},{20... | collective-permute-start | bytes 491528 | tf_op jit(solution)/shard_map/ppermute | solution.py:77
  12.1 2.7 %collective-permute-done = bf16[64,1280]{1,0:T(8,128)(2,1)S(1)} collective-permute-done((bf16[64,1280]{1,0:T(8,128)(2,1)S(1)}, bf16[64,1280]{1,0:T(8,128)(2,1)S(1)}, u32[]{:S(2)}, u32[]{:S(2)}) %collective-permute-start) | collective-permute-done | bytes 163872 | tf_op jit(solution)/shard_map/ppermute | solution.py:77
  14.8 1.8 maximum_select_fusion
  16.6 79.7 %all-gather.2.cloned.1.call-done = bf16[2048,1280]{1,0:T(8,128)(2,1)} async-done(((bf16[128,1280]{1,0:T(8,128)(2,1)}), bf16[2048,1280]{1,0:T(8,128)(2,1)}) %all-gather.2.cloned.1.call-update) | async-done | bytes 5242896 | tf_op jit(solution)/shard_map/all_gather | solution.py:82
  96.3 10.1 %collective-permute-start.1 = (bf16[2048,1280]{1,0:T(8,128)(2,1)}, bf16[2048,1280]{1,0:T(8,128)(2,1)}, u32[]{:S(2)}, u32[]{:S(2)}) collective-permute-start(bf16[2048,1280]{1,0:T(8,128)(2,1)} %all-gather.2.cloned.1.call-done), channel_id=1, source_target_pairs={{0,8},{8,0},{1,9},{9,1},{2,10},{10,2},{3,11},{11,3},{4,12},{12,4},... | collective-permute-start | bytes 15728648 | tf_op jit(solution)/shard_map/ppermute | solution.py:83
  106.4 0.7 convert_element_type.61
  107.1 1.1 fusion.15
  108.2 1.1 fusion.17
  110.8 1.5 broadcast_in_dim.16
  112.3 6.4 %all-to-all-start = ((bf16[8,32,4096]{2,1,0:T(8,128)(2,1)}), bf16[8,32,4096]{2,1,0:T(8,128)(2,1)S(1)}, u32[]{:S(2)}, u32[]{:S(2)}) async-start(bf16[8,32,4096]{2,1,0:T(8,128)(2,1)} %broadcast_in_dim.16), calls=%async_computation | async-start | bytes 4194304 | tf_op jit(solution)/shard_map/all_to_all | solution.py:73
  120.2 26.8 %all-to-all-done = bf16[8,32,4096]{2,1,0:T(8,128)(2,1)S(1)} async-done(((bf16[8,32,4096]{2,1,0:T(8,128)(2,1)}), bf16[8,32,4096]{2,1,0:T(8,128)(2,1)S(1)}, u32[]{:S(2)}, u32[]{:S(2)}) %all-to-all-start) | async-done | bytes 2097184 | tf_op jit(solution)/shard_map/all_to_all | solution.py:73
  147.0 2.9 %fusion = f32[256,768]{1,0:T(8,128)S(1)} fusion(bf16[2048,1280]{1,0:T(8,128)(2,1)} %collective-permute-done.1, bf16[256,4096]{1,0:T(8,128)(2,1)S(1)} %bitcast.89), kind=kOutput, calls=%fused_computation.1 | convolution fusion | flops 805306368 | bytes 4980736 | tf_op jit(solution)/shard_map/dot_general | solution.py:88
  149.8 2.9 %fusion.5 = f32[256,768]{1,0:T(8,128)S(1)} fusion(f32[256,768]{1,0:T(8,128)S(1)} %fusion, bf16[2048,1280]{1,0:T(8,128)(2,1)} %all-gather.2.cloned.1.call-done, bf16[256,4096]{1,0:T(8,128)(2,1)S(1)} %bitcast.90), kind=kOutput, calls=%fused_computation.12 | convolution fusion | flops 805502976 | bytes 5767168 | tf_op jit(solution)/shard_map/dot_general | solution.py:86
  155.3 2.3 %convolution_convert_fusion.1 = bf16[8,32,2048]{2,1,0:T(8,128)(2,1)S(1)} fusion(bf16[8,32,512]{2,1,0:T(8,128)(2,1)S(1)} %dot_general.24, bf16[2048,1280]{1,0:T(8,128)(2,1)} %all-gather.2.cloned.1.call-done), kind=kOutput, calls=%fused_computation.6 | convolution fusion | flops 537395200 | bytes 3407872 | tf_op jit(solution)/shard_map/dot_general | solution.py:127
  157.7 2.3 %convolution_convert_fusion = bf16[8,32,2048]{2,1,0:T(8,128)(2,1)S(1)} fusion(bf16[8,32,512]{2,1,0:T(8,128)(2,1)S(1)} %dot_general.24, bf16[2048,1280]{1,0:T(8,128)(2,1)} %collective-permute-done.1), kind=kOutput, calls=%fused_computation.5 | convolution fusion | flops 537395200 | bytes 3407872 | tf_op jit(solution)/shard_map/dot_general | solution.py:128
  160.0 1.6 pad_maximum_fusion
  161.6 3.8 %all-to-all-start.1 = ((bf16[8,32,4096]{2,1,0:T(8,128)(2,1)}), bf16[8,32,4096]{2,1,0:T(8,128)(2,1)S(1)}, u32[]{:S(2)}, u32[]{:S(2)}) async-start(bf16[8,32,4096]{2,1,0:T(8,128)(2,1)} %pad_maximum_fusion), calls=%async_computation.1 | async-start | bytes 4194304 | tf_op jit(solution)/shard_map/all_to_all | solution.py:132
  166.1 26.4 %all-to-all-done.1 = bf16[8,32,4096]{2,1,0:T(8,128)(2,1)S(1)} async-done(((bf16[8,32,4096]{2,1,0:T(8,128)(2,1)}), bf16[8,32,4096]{2,1,0:T(8,128)(2,1)S(1)}, u32[]{:S(2)}, u32[]{:S(2)}) %all-to-all-start.1) | async-done | bytes 2097184 | tf_op jit(solution)/shard_map/all_to_all | solution.py:132
  193.2 0.8 fusion.21
  194.3 0.8 reshape.159
  195.1 0.8 copy.21
  195.9 0.9 reshape.160
  196.9 0.8 fusion.18
  (42 shorter events, 7.2 us)
Async XLA Ops:
  7.2 89.1 %all-gather.2.cloned.1.call-start = ((), (), s32[]{:S(2)}) async-start(), calls=%async_computation.2 | async-start | bytes 5570560 | tf_op jit(solution)/shard_map/all_gather | solution.py:82
  8.1 6.6 %collective-permute-start = (bf16[64,1280]{1,0:T(8,128)(2,1)S(1)}, bf16[64,1280]{1,0:T(8,128)(2,1)S(1)}, u32[]{:S(2)}, u32[]{:S(2)}) collective-permute-start(bf16[64,1280]{1,0:T(8,128)(2,1)S(1)} %pad_maximum_fusion.1), channel_id=1, source_target_pairs={{0,16},{16,0},{1,17},{17,1},{2,18},{18,2},{3,19},{19,3},{4,20},{20... | collective-permute-start | bytes 491528 | tf_op jit(solution)/shard_map/ppermute | solution.py:77
  96.3 50.7 %collective-permute-start.1 = (bf16[2048,1280]{1,0:T(8,128)(2,1)}, bf16[2048,1280]{1,0:T(8,128)(2,1)}, u32[]{:S(2)}, u32[]{:S(2)}) collective-permute-start(bf16[2048,1280]{1,0:T(8,128)(2,1)} %all-gather.2.cloned.1.call-done), channel_id=1, source_target_pairs={{0,8},{8,0},{1,9},{9,1},{2,10},{10,2},{3,11},{11,3},{4,12},{12,4},... | collective-permute-start | bytes 15728648 | tf_op jit(solution)/shard_map/ppermute | solution.py:83
  110.8 8.0 %copy-start.1 = (s32[256]{0:T(256)S(1)}, s32[256]{0:T(256)}, u32[]{:S(2)}) copy-start(s32[256]{0:T(256)} %param.13) | copy-start | bytes 3076
  112.3 34.7 %all-to-all-start = ((bf16[8,32,4096]{2,1,0:T(8,128)(2,1)}), bf16[8,32,4096]{2,1,0:T(8,128)(2,1)S(1)}, u32[]{:S(2)}, u32[]{:S(2)}) async-start(bf16[8,32,4096]{2,1,0:T(8,128)(2,1)} %broadcast_in_dim.16), calls=%async_computation | async-start | bytes 4194304 | tf_op jit(solution)/shard_map/all_to_all | solution.py:73
  161.6 30.9 %all-to-all-start.1 = ((bf16[8,32,4096]{2,1,0:T(8,128)(2,1)}), bf16[8,32,4096]{2,1,0:T(8,128)(2,1)S(1)}, u32[]{:S(2)}, u32[]{:S(2)}) async-start(bf16[8,32,4096]{2,1,0:T(8,128)(2,1)} %pad_maximum_fusion), calls=%async_computation.1 | async-start | bytes 4194304 | tf_op jit(solution)/shard_map/all_to_all | solution.py:132
  194.0 2.9 %copy-start = (bf16[32,4096]{1,0:T(8,128)(2,1)S(1)}, bf16[32,4096]{1,0:T(8,128)(2,1)}, u32[]{:S(2)}) copy-start(bf16[32,4096]{1,0:T(8,128)(2,1)} %param.7) | copy-start | bytes 786436
Sparse Core Ops, SparseCore 0:
  16.7 79.5 all-gather.1

commit v6 on v5

--- a/solution.py
+++ b/solution.py
@@ -66,19 +66,18 @@
     normed = rms_normed(rows_float, norm_gain)
     tensor_size = pack_rows // normed.shape[0]
     core = lax.axis_index("c")
+    pair_side = lax.axis_index("xl")
     split_d = normed.reshape(normed.shape[0], -1, 2, 2, packed_rows)
-    by_core = jnp.transpose(split_d, (0, 3, 1, 2, 4)).reshape(normed.shape[0], 2, -1)
+    by_core = jnp.transpose(split_d, (0, 3, 1, 2, 4))
     by_core = lax.dynamic_slice_in_dim(jnp.concatenate((by_core, by_core), axis=1), core, 2, axis=1)
+    by_core = lax.dynamic_slice_in_dim(jnp.concatenate((by_core, by_core), axis=3), pair_side, 2, axis=3)
     normed = by_core.reshape(normed.shape)
     gathered = lax.all_to_all(
         jnp.broadcast_to(normed[None], (tensor_size,) + normed.shape), "tensor", 0, 0, tiled=True
     ).reshape(pack_rows, normed.shape[1])
     packed = jnp.concatenate((w_query, w_key, w_value, w_out.T), axis=1)
     pair = lax.ppermute(packed, "xl", [(0, 1), (1, 0)])
-    first_xl = lax.axis_index("xl") == 0
-    chip_pair = jnp.where(
-        first_xl, jnp.concatenate((packed, pair)), jnp.concatenate((pair, packed))
-    )
+    chip_pair = jnp.concatenate((packed, pair))
     core_half = lax.all_gather(chip_pair, "z", axis=0, tiled=True)
     other_half = lax.ppermute(core_half, "c", [(0, 1), (1, 0)])
     half_rows = core_half.shape[0]
@@ -133,9 +132,9 @@
         out_rows.astype(jnp.bfloat16).reshape(tensor_size, -1, out_rows.shape[1]), "tensor", 0, 0, tiled=True
     )
     summed = jnp.sum(pieces.astype(jnp.float32), axis=0)
-    split_s = summed.reshape(summed.shape[0], 2, -1)
+    split_s = summed.reshape(summed.shape[0], 2, -1, 2, packed_rows)
     split_s = lax.dynamic_slice_in_dim(jnp.concatenate((split_s, split_s), axis=1), core, 2, axis=1)
-    split_s = split_s.reshape(summed.shape[0], 2, -1, 2, packed_rows)
+    split_s = lax.dynamic_slice_in_dim(jnp.concatenate((split_s, split_s), axis=3), pair_side, 2, axis=3)
     summed = jnp.transpose(split_s, (0, 2, 3, 1, 4)).reshape(summed.shape)
     hidden_out = (summed + rows_float).astype(jnp.bfloat16)
     return (hidden_out, cache_rows)

time: 205 us -> 210 us (1.024)
  other arithmetic: 12.2 us -> 18 us
    concatenate x0 -> x3, other arithmetic: none -> 5.54 us  [the longest x1 2.31 us: layer(): jnp.concatenate((by_core, by_core), axis=3)]
  transfers between devices with their start and end apart: 5 -> 5, of which waited for: 4 -> 4; matrix products, arithmetic and copies ran while one was open for 4% -> 6% of each run, Pallas kernels for 0% -> 0%
where the time goes in v6:
time: 210 us
  waiting for transfers between devices  136 us (65%)
  starting transfers between devices  24.4 us (12%)
  other arithmetic  18 us (9%)
  between operations  14.3 us (7%)
  matrix products  11.1 us (5%)
  local copies, waits for them, and re-layouts  6.33 us (3%)
    all_gather x1, waiting for transfers between devices, layer(): core_half = lax.all_gather(chip_pair, 'z', axis=0, tiled=True)  79.7 us
    all_to_all x1, waiting for transfers between devices, layer(): lax.all_to_all(jnp.broadcast_to(normed[None], (tensor_size,) + normed.sha...  26.8 us
    all_to_all x1, waiting for transfers between devices, layer(): lax.all_to_all(out_rows.astype(jnp.bfloat16).reshape(tensor_size, -1, out...  26.4 us
    ppermute x1, starting transfers between devices, layer(): other_half = lax.ppermute(core_half, 'c', [(0, 1), (1, 0)])  10.1 us
    all_to_all x1, starting transfers between devices, layer(): lax.all_to_all(jnp.broadcast_to(normed[None], (tensor_size,) + normed.sha...  6.55 us
  transfers between devices with their start and end apart: 5, of which 4 were waited for; matrix products, arithmetic and copies ran while one was open for 6% of the time, Pallas kernels for 0%

profile of v6, /device:TPU:1, one launch (start us, length us, event | category | flops | bytes accessed | tf_op | source)
XLA Modules:
  0.0 209.8 jit_solution(2887104472247727852)
XLA Ops:
  7.2 0.9 pad_maximum_fusion.2
  8.1 3.9 %collective-permute-start = (bf16[64,1280]{1,0:T(8,128)(2,1)S(1)}, bf16[64,1280]{1,0:T(8,128)(2,1)S(1)}, u32[]{:S(2)}, u32[]{:S(2)}) collective-permute-start(bf16[64,1280]{1,0:T(8,128)(2,1)S(1)} %pad_maximum_fusion.2), channel_id=1, source_target_pairs={{0,16},{16,0},{1,17},{17,1},{2,18},{18,2},{3,19},{19,3},{4,20},{20... | collective-permute-start | bytes 491528 | tf_op jit(solution)/shard_map/ppermute | solution.py:79
  12.1 2.7 %collective-permute-done = bf16[64,1280]{1,0:T(8,128)(2,1)S(1)} collective-permute-done((bf16[64,1280]{1,0:T(8,128)(2,1)S(1)}, bf16[64,1280]{1,0:T(8,128)(2,1)S(1)}, u32[]{:S(2)}, u32[]{:S(2)}) %collective-permute-start) | collective-permute-done | bytes 163872 | tf_op jit(solution)/shard_map/ppermute | solution.py:79
  14.8 1.7 pad_maximum_fusion.1
  16.5 79.7 %all-gather.2.cloned.1.call-done = bf16[2048,1280]{1,0:T(8,128)(2,1)} async-done(((bf16[128,1280]{1,0:T(8,128)(2,1)}), bf16[2048,1280]{1,0:T(8,128)(2,1)}) %all-gather.2.cloned.1.call-update) | async-done | bytes 5242896 | tf_op jit(solution)/shard_map/all_gather | solution.py:81
  96.2 10.1 %collective-permute-start.1 = (bf16[2048,1280]{1,0:T(8,128)(2,1)}, bf16[2048,1280]{1,0:T(8,128)(2,1)}, u32[]{:S(2)}, u32[]{:S(2)}) collective-permute-start(bf16[2048,1280]{1,0:T(8,128)(2,1)} %all-gather.2.cloned.1.call-done), channel_id=1, source_target_pairs={{0,8},{8,0},{1,9},{9,1},{2,10},{10,2},{3,11},{11,3},{4,12},{12,4},... | collective-permute-start | bytes 15728648 | tf_op jit(solution)/shard_map/ppermute | solution.py:82
  107.0 1.1 fusion.19
  108.1 1.1 fusion.21
  110.1 1.6 fusion.18
  111.7 2.3 %fusion.25 = bf16[32,2,16,2,64]{4,3,2,1,0:T(2,128)(2,1)S(1)} fusion(s32[]{:T(128)S(6)} %select_n.35, bf16[32,2,16,2,64]{4,3,2,1,0:T(2,128)(2,1)S(1)} %fusion.18), kind=kLoop, calls=%fused_computation.42 | loop fusion | flops 524288 | bytes 524292 | tf_op jit(solution)/shard_map/concatenate | solution.py:73
  114.5 1.5 broadcast_in_dim.16
  116.0 6.6 %all-to-all-start = ((bf16[8,32,4096]{2,1,0:T(8,128)(2,1)}), bf16[8,32,4096]{2,1,0:T(8,128)(2,1)S(1)}, u32[]{:S(2)}, u32[]{:S(2)}) async-start(bf16[8,32,4096]{2,1,0:T(8,128)(2,1)} %broadcast_in_dim.16), calls=%async_computation | async-start | bytes 4194304 | tf_op jit(solution)/shard_map/all_to_all | solution.py:75
  124.0 26.8 %all-to-all-done = bf16[8,32,4096]{2,1,0:T(8,128)(2,1)S(1)} async-done(((bf16[8,32,4096]{2,1,0:T(8,128)(2,1)}), bf16[8,32,4096]{2,1,0:T(8,128)(2,1)S(1)}, u32[]{:S(2)}, u32[]{:S(2)}) %all-to-all-start) | async-done | bytes 2097184 | tf_op jit(solution)/shard_map/all_to_all | solution.py:75
  150.8 2.9 %fusion = f32[256,768]{1,0:T(8,128)S(1)} fusion(bf16[2048,1280]{1,0:T(8,128)(2,1)} %collective-permute-done.1, bf16[256,4096]{1,0:T(8,128)(2,1)S(1)} %bitcast.82), kind=kOutput, calls=%fused_computation.1 | convolution fusion | flops 805306368 | bytes 4980736 | tf_op jit(solution)/shard_map/dot_general | solution.py:87
  153.7 2.9 %fusion.5 = f32[256,768]{1,0:T(8,128)S(1)} fusion(f32[256,768]{1,0:T(8,128)S(1)} %fusion, bf16[2048,1280]{1,0:T(8,128)(2,1)} %all-gather.2.cloned.1.call-done, bf16[256,4096]{1,0:T(8,128)(2,1)S(1)} %bitcast.83), kind=kOutput, calls=%fused_computation.16 | convolution fusion | flops 805502976 | bytes 5767168 | tf_op jit(solution)/shard_map/dot_general | solution.py:85
  159.1 2.3 %convolution_convert_fusion.1 = bf16[8,32,2048]{2,1,0:T(8,128)(2,1)S(1)} fusion(bf16[8,32,512]{2,1,0:T(8,128)(2,1)S(1)} %dot_general.24, bf16[2048,1280]{1,0:T(8,128)(2,1)} %all-gather.2.cloned.1.call-done), kind=kOutput, calls=%fused_computation.6 | convolution fusion | flops 537395200 | bytes 3407872 | tf_op jit(solution)/shard_map/dot_general | solution.py:126
  161.5 2.3 %convolution_convert_fusion = bf16[8,32,2048]{2,1,0:T(8,128)(2,1)S(1)} fusion(bf16[8,32,512]{2,1,0:T(8,128)(2,1)S(1)} %dot_general.24, bf16[2048,1280]{1,0:T(8,128)(2,1)} %collective-permute-done.1), kind=kOutput, calls=%fused_computation.5 | convolution fusion | flops 537395200 | bytes 3407872 | tf_op jit(solution)/shard_map/dot_general | solution.py:127
  163.8 1.6 pad_maximum_fusion
  165.4 3.8 %all-to-all-start.1 = ((bf16[8,32,4096]{2,1,0:T(8,128)(2,1)}), bf16[8,32,4096]{2,1,0:T(8,128)(2,1)S(1)}, u32[]{:S(2)}, u32[]{:S(2)}) async-start(bf16[8,32,4096]{2,1,0:T(8,128)(2,1)} %pad_maximum_fusion), calls=%async_computation.1 | async-start | bytes 4194304 | tf_op jit(solution)/shard_map/all_to_all | solution.py:131
  169.9 26.4 %all-to-all-done.1 = bf16[8,32,4096]{2,1,0:T(8,128)(2,1)S(1)} async-done(((bf16[8,32,4096]{2,1,0:T(8,128)(2,1)}), bf16[8,32,4096]{2,1,0:T(8,128)(2,1)S(1)}, u32[]{:S(2)}, u32[]{:S(2)}) %all-to-all-start.1) | async-done | bytes 2097184 | tf_op jit(solution)/shard_map/all_to_all | solution.py:131
  197.4 1.1 fusion.13
  198.5 1.9 fusion.12
  200.4 0.8 copy.19
  201.2 0.9 reshape.152
  (41 shorter events, 8.6 us)
Async XLA Ops:
  7.2 89.0 %all-gather.2.cloned.1.call-start = ((), (), s32[]{:S(2)}) async-start(), calls=%async_computation.2 | async-start | bytes 5570560 | tf_op jit(solution)/shard_map/all_gather | solution.py:81
  8.1 6.6 %collective-permute-start = (bf16[64,1280]{1,0:T(8,128)(2,1)S(1)}, bf16[64,1280]{1,0:T(8,128)(2,1)S(1)}, u32[]{:S(2)}, u32[]{:S(2)}) collective-permute-start(bf16[64,1280]{1,0:T(8,128)(2,1)S(1)} %pad_maximum_fusion.2), channel_id=1, source_target_pairs={{0,16},{16,0},{1,17},{17,1},{2,18},{18,2},{3,19},{19,3},{4,20},{20... | collective-permute-start | bytes 491528 | tf_op jit(solution)/shard_map/ppermute | solution.py:79
  96.2 54.6 %collective-permute-start.1 = (bf16[2048,1280]{1,0:T(8,128)(2,1)}, bf16[2048,1280]{1,0:T(8,128)(2,1)}, u32[]{:S(2)}, u32[]{:S(2)}) collective-permute-start(bf16[2048,1280]{1,0:T(8,128)(2,1)} %all-gather.2.cloned.1.call-done), channel_id=1, source_target_pairs={{0,8},{8,0},{1,9},{9,1},{2,10},{10,2},{3,11},{11,3},{4,12},{12,4},... | collective-permute-start | bytes 15728648 | tf_op jit(solution)/shard_map/ppermute | solution.py:82
  116.0 6.6 %copy-start.1 = (s32[256]{0:T(256)S(1)}, s32[256]{0:T(256)}, u32[]{:S(2)}) copy-start(s32[256]{0:T(256)} %param.13) | copy-start | bytes 3076
  116.0 34.8 %all-to-all-start = ((bf16[8,32,4096]{2,1,0:T(8,128)(2,1)}), bf16[8,32,4096]{2,1,0:T(8,128)(2,1)S(1)}, u32[]{:S(2)}, u32[]{:S(2)}) async-start(bf16[8,32,4096]{2,1,0:T(8,128)(2,1)} %broadcast_in_dim.16), calls=%async_computation | async-start | bytes 4194304 | tf_op jit(solution)/shard_map/all_to_all | solution.py:75
  165.4 30.9 %all-to-all-start.1 = ((bf16[8,32,4096]{2,1,0:T(8,128)(2,1)}), bf16[8,32,4096]{2,1,0:T(8,128)(2,1)S(1)}, u32[]{:S(2)}, u32[]{:S(2)}) async-start(bf16[8,32,4096]{2,1,0:T(8,128)(2,1)} %pad_maximum_fusion), calls=%async_computation.1 | async-start | bytes 4194304 | tf_op jit(solution)/shard_map/all_to_all | solution.py:131
  200.4 1.8 copy-start
Sparse Core Ops, SparseCore 0:
  16.6 79.5 all-gather.1

commit v7 on v5

--- a/solution.py
+++ b/solution.py
@@ -122,17 +122,14 @@
         jnp.transpose(mixed_rows, (2, 0, 1, 3)).astype(jnp.bfloat16).reshape(pack_rows, query_cols)
     )
     out_dims = (((1,), (1,)), ((), ()))
-    out_rows = jnp.concatenate(
-        (
-            lax.dot_general(attended, core_half[:, proj_cols:], out_dims, preferred_element_type=jnp.float32),
-            lax.dot_general(attended, other_half[:, proj_cols:], out_dims, preferred_element_type=jnp.float32),
-        ),
-        axis=1,
-    )
-    pieces = lax.all_to_all(
-        out_rows.astype(jnp.bfloat16).reshape(tensor_size, -1, out_rows.shape[1]), "tensor", 0, 0, tiled=True
-    )
-    summed = jnp.sum(pieces.astype(jnp.float32), axis=0)
+    sums = []
+    for out_half in (core_half[:, proj_cols:], other_half[:, proj_cols:]):
+        part = lax.dot_general(attended, out_half, out_dims, preferred_element_type=jnp.float32)
+        got = lax.all_to_all(
+            part.astype(jnp.bfloat16).reshape(tensor_size, -1, part.shape[1]), "tensor", 0, 0, tiled=True
+        )
+        sums.append(jnp.sum(got.astype(jnp.float32), axis=0))
+    summed = jnp.concatenate(sums, axis=1)
     split_s = summed.reshape(summed.shape[0], 2, -1)
     split_s = lax.dynamic_slice_in_dim(jnp.concatenate((split_s, split_s), axis=1), core, 2, axis=1)
     split_s = split_s.reshape(summed.shape[0], 2, -1, 2, packed_rows)

time: 205 us -> 210 us (1.024)
  starting transfers between devices: 24.3 us -> 28.2 us
    all_to_all x1 -> x2, starting transfers between devices: 3.78 us -> 7.68 us  [layer(): lax.all_to_all(part.astype(jnp.bfloat16).reshape(tensor_size, -1, part.sh...]
    all_to_all x1 -> x2, waiting for transfers between devices: 26.4 us -> 26.9 us  [layer(): lax.all_to_all(part.astype(jnp.bfloat16).reshape(tensor_size, -1, part.sh...]
  transfers between devices with their start and end apart: 5 -> 6, of which waited for: 4 -> 5; matrix products, arithmetic and copies ran while one was open for 4% -> 5% of each run, Pallas kernels for 0% -> 0%
where the time goes in v7:
time: 210 us; the launch traced here: 209 us
  waiting for transfers between devices  136 us (65%)
  starting transfers between devices  28.2 us (13%)
  between operations  14.3 us (7%)
  matrix products  13.1 us (6%)
  other arithmetic  10.6 us (5%)
  local copies, waits for them, and re-layouts  6.7 us (3%)
    all_gather x1, waiting for transfers between devices, layer(): core_half = lax.all_gather(chip_pair, 'z', axis=0, tiled=True)  79.7 us
    all_to_all x2, waiting for transfers between devices, layer(): lax.all_to_all(part.astype(jnp.bfloat16).reshape(tensor_size, -1, part.sh...  26.9 us
    all_to_all x1, waiting for transfers between devices, layer(): lax.all_to_all(jnp.broadcast_to(normed[None], (tensor_size,) + normed.sha...  26.8 us
    ppermute x1, starting transfers between devices, layer(): other_half = lax.ppermute(core_half, 'c', [(0, 1), (1, 0)])  10.1 us
    all_to_all x2, starting transfers between devices, layer(): lax.all_to_all(part.astype(jnp.bfloat16).reshape(tensor_size, -1, part.sh...  7.68 us
    dot_general x2, matrix products, layer(): lax.dot_general(attended, out_half, out_dims, preferred_element_type=jnp....  6.68 us
    all_to_all x1, starting transfers between devices, layer(): lax.all_to_all(jnp.broadcast_to(normed[None], (tensor_size,) + normed.sha...  6.42 us
  transfers between devices with their start and end apart: 6, of which 5 were waited for; matrix products, arithmetic and copies ran while one was open for 5% of the time, Pallas kernels for 0%

profile of v7, /device:TPU:1, one launch (start us, length us, event | category | flops | bytes accessed | tf_op | source)
XLA Modules:
  0.0 208.9 jit_solution(2227169750965944392)
XLA Ops:
  7.2 0.9 pad_maximum_fusion.1
  8.1 3.9 %collective-permute-start = (bf16[64,1280]{1,0:T(8,128)(2,1)S(1)}, bf16[64,1280]{1,0:T(8,128)(2,1)S(1)}, u32[]{:S(2)}, u32[]{:S(2)}) collective-permute-start(bf16[64,1280]{1,0:T(8,128)(2,1)S(1)} %pad_maximum_fusion.1), channel_id=1, source_target_pairs={{0,16},{16,0},{1,17},{17,1},{2,18},{18,2},{3,19},{19,3},{4,20},{20... | collective-permute-start | bytes 491528 | tf_op jit(solution)/shard_map/ppermute | solution.py:77
  12.1 2.7 %collective-permute-done = bf16[64,1280]{1,0:T(8,128)(2,1)S(1)} collective-permute-done((bf16[64,1280]{1,0:T(8,128)(2,1)S(1)}, bf16[64,1280]{1,0:T(8,128)(2,1)S(1)}, u32[]{:S(2)}, u32[]{:S(2)}) %collective-permute-start) | collective-permute-done | bytes 163872 | tf_op jit(solution)/shard_map/ppermute | solution.py:77
  14.8 1.8 maximum_select_fusion
  16.6 79.7 %all-gather.2.cloned.1.call-done = bf16[2048,1280]{1,0:T(8,128)(2,1)} async-done(((bf16[128,1280]{1,0:T(8,128)(2,1)}), bf16[2048,1280]{1,0:T(8,128)(2,1)}) %all-gather.2.cloned.1.call-update) | async-done | bytes 5242896 | tf_op jit(solution)/shard_map/all_gather | solution.py:82
  96.3 10.1 %collective-permute-start.1 = (bf16[2048,1280]{1,0:T(8,128)(2,1)}, bf16[2048,1280]{1,0:T(8,128)(2,1)}, u32[]{:S(2)}, u32[]{:S(2)}) collective-permute-start(bf16[2048,1280]{1,0:T(8,128)(2,1)} %all-gather.2.cloned.1.call-done), channel_id=1, source_target_pairs={{0,8},{8,0},{1,9},{9,1},{2,10},{10,2},{3,11},{11,3},{4,12},{12,4},... | collective-permute-start | bytes 15728648 | tf_op jit(solution)/shard_map/ppermute | solution.py:83
  107.1 1.1 fusion.16
  108.2 1.1 fusion.18
  110.8 1.5 broadcast_in_dim.16
  112.3 6.4 %all-to-all-start = ((bf16[8,32,4096]{2,1,0:T(8,128)(2,1)}), bf16[8,32,4096]{2,1,0:T(8,128)(2,1)S(1)}, u32[]{:S(2)}, u32[]{:S(2)}) async-start(bf16[8,32,4096]{2,1,0:T(8,128)(2,1)} %broadcast_in_dim.16), calls=%async_computation | async-start | bytes 4194304 | tf_op jit(solution)/shard_map/all_to_all | solution.py:73
  120.2 26.8 %all-to-all-done = bf16[8,32,4096]{2,1,0:T(8,128)(2,1)S(1)} async-done(((bf16[8,32,4096]{2,1,0:T(8,128)(2,1)}), bf16[8,32,4096]{2,1,0:T(8,128)(2,1)S(1)}, u32[]{:S(2)}, u32[]{:S(2)}) %all-to-all-start) | async-done | bytes 2097184 | tf_op jit(solution)/shard_map/all_to_all | solution.py:73
  147.0 2.9 %fusion = f32[256,768]{1,0:T(8,128)S(1)} fusion(bf16[2048,1280]{1,0:T(8,128)(2,1)} %collective-permute-done.1, bf16[256,4096]{1,0:T(8,128)(2,1)S(1)} %bitcast.84), kind=kOutput, calls=%fused_computation | convolution fusion | flops 805306368 | bytes 4980736 | tf_op jit(solution)/shard_map/dot_general | solution.py:88
  149.8 2.9 %fusion.7 = f32[256,768]{1,0:T(8,128)S(1)} fusion(f32[256,768]{1,0:T(8,128)S(1)} %fusion, bf16[2048,1280]{1,0:T(8,128)(2,1)} %all-gather.2.cloned.1.call-done, bf16[256,4096]{1,0:T(8,128)(2,1)S(1)} %bitcast.85), kind=kOutput, calls=%fused_computation.12 | convolution fusion | flops 805502976 | bytes 5767168 | tf_op jit(solution)/shard_map/dot_general | solution.py:86
  154.9 3.3 %convolution_convert_fusion.1 = bf16[256,2048]{1,0:T(8,128)(2,1)} fusion(bf16[256,512]{0,1:T(8,128)(2,1)S(1)} %bitcast.94, bf16[2048,1280]{1,0:T(8,128)(2,1)} %all-gather.2.cloned.1.call-done), kind=kOutput, calls=%fused_computation.5 | convolution fusion | flops 537395200 | bytes 3407872 | tf_op jit(solution)/shard_map/dot_general | solution.py:127
  158.3 3.6 %all-to-all-start.1 = ((bf16[8,32,2048]{2,1,0:T(8,128)(2,1)}), bf16[8,32,2048]{2,1,0:T(8,128)(2,1)S(1)}, u32[]{:S(2)}, u32[]{:S(2)}) async-start(bf16[8,32,2048]{2,1,0:T(8,128)(2,1)} %bitcast.16), calls=%async_computation.1 | async-start | bytes 2097152 | tf_op jit(solution)/shard_map/all_to_all | solution.py:128
  161.8 3.3 %convolution_convert_fusion = bf16[256,2048]{1,0:T(8,128)(2,1)} fusion(bf16[256,512]{0,1:T(8,128)(2,1)S(1)} %bitcast.95, bf16[2048,1280]{1,0:T(8,128)(2,1)} %collective-permute-done.1), kind=kOutput, calls=%fused_computation.4 | convolution fusion | flops 537395200 | bytes 3407872 | tf_op jit(solution)/shard_map/dot_general | solution.py:127
  165.2 12.4 %all-to-all-done.1 = bf16[8,32,2048]{2,1,0:T(8,128)(2,1)S(1)} async-done(((bf16[8,32,2048]{2,1,0:T(8,128)(2,1)}), bf16[8,32,2048]{2,1,0:T(8,128)(2,1)S(1)}, u32[]{:S(2)}, u32[]{:S(2)}) %all-to-all-start.1) | async-done | bytes 1048608 | tf_op jit(solution)/shard_map/all_to_all | solution.py:128
  177.6 4.1 %all-to-all-start.2 = ((bf16[8,32,2048]{2,1,0:T(8,128)(2,1)}), bf16[8,32,2048]{2,1,0:T(8,128)(2,1)S(1)}, u32[]{:S(2)}, u32[]{:S(2)}) async-start(bf16[8,32,2048]{2,1,0:T(8,128)(2,1)} %bitcast.90), calls=%async_computation.2 | async-start | bytes 2097152 | tf_op jit(solution)/shard_map/all_to_all | solution.py:128
  182.5 14.4 %all-to-all-done.2 = bf16[8,32,2048]{2,1,0:T(8,128)(2,1)S(1)} async-done(((bf16[8,32,2048]{2,1,0:T(8,128)(2,1)}), bf16[8,32,2048]{2,1,0:T(8,128)(2,1)S(1)}, u32[]{:S(2)}, u32[]{:S(2)}) %all-to-all-start.2) | async-done | bytes 1048608 | tf_op jit(solution)/shard_map/all_to_all | solution.py:128
  197.6 0.8 fusion.22
  198.7 0.8 reshape.163
  199.5 0.8 copy.22
  200.3 0.9 reshape.164
  201.3 0.8 fusion.19
  (43 shorter events, 7.5 us)
Async XLA Ops:
  7.2 89.1 %all-gather.2.cloned.1.call-start = ((), (), s32[]{:S(2)}) async-start(), calls=%async_computation.3 | async-start | bytes 5570560 | tf_op jit(solution)/shard_map/all_gather | solution.py:82
  8.1 6.6 %collective-permute-start = (bf16[64,1280]{1,0:T(8,128)(2,1)S(1)}, bf16[64,1280]{1,0:T(8,128)(2,1)S(1)}, u32[]{:S(2)}, u32[]{:S(2)}) collective-permute-start(bf16[64,1280]{1,0:T(8,128)(2,1)S(1)} %pad_maximum_fusion.1), channel_id=1, source_target_pairs={{0,16},{16,0},{1,17},{17,1},{2,18},{18,2},{3,19},{19,3},{4,20},{20... | collective-permute-start | bytes 491528 | tf_op jit(solution)/shard_map/ppermute | solution.py:77
  96.3 50.7 %collective-permute-start.1 = (bf16[2048,1280]{1,0:T(8,128)(2,1)}, bf16[2048,1280]{1,0:T(8,128)(2,1)}, u32[]{:S(2)}, u32[]{:S(2)}) collective-permute-start(bf16[2048,1280]{1,0:T(8,128)(2,1)} %all-gather.2.cloned.1.call-done), channel_id=1, source_target_pairs={{0,8},{8,0},{1,9},{9,1},{2,10},{10,2},{3,11},{11,3},{4,12},{12,4},... | collective-permute-start | bytes 15728648 | tf_op jit(solution)/shard_map/ppermute | solution.py:83
  110.8 8.0 %copy-start.1 = (s32[256]{0:T(256)S(1)}, s32[256]{0:T(256)}, u32[]{:S(2)}) copy-start(s32[256]{0:T(256)} %param.13) | copy-start | bytes 3076
  112.3 34.7 %all-to-all-start = ((bf16[8,32,4096]{2,1,0:T(8,128)(2,1)}), bf16[8,32,4096]{2,1,0:T(8,128)(2,1)S(1)}, u32[]{:S(2)}, u32[]{:S(2)}) async-start(bf16[8,32,4096]{2,1,0:T(8,128)(2,1)} %broadcast_in_dim.16), calls=%async_computation | async-start | bytes 4194304 | tf_op jit(solution)/shard_map/all_to_all | solution.py:73
  158.3 19.3 %all-to-all-start.1 = ((bf16[8,32,2048]{2,1,0:T(8,128)(2,1)}), bf16[8,32,2048]{2,1,0:T(8,128)(2,1)S(1)}, u32[]{:S(2)}, u32[]{:S(2)}) async-start(bf16[8,32,2048]{2,1,0:T(8,128)(2,1)} %bitcast.16), calls=%async_computation.1 | async-start | bytes 2097152 | tf_op jit(solution)/shard_map/all_to_all | solution.py:128
  177.6 19.4 %all-to-all-start.2 = ((bf16[8,32,2048]{2,1,0:T(8,128)(2,1)}), bf16[8,32,2048]{2,1,0:T(8,128)(2,1)S(1)}, u32[]{:S(2)}, u32[]{:S(2)}) async-start(bf16[8,32,2048]{2,1,0:T(8,128)(2,1)} %bitcast.90), calls=%async_computation.2 | async-start | bytes 2097152 | tf_op jit(solution)/shard_map/all_to_all | solution.py:128
  198.4 2.9 %copy-start = (bf16[32,4096]{1,0:T(8,128)(2,1)S(1)}, bf16[32,4096]{1,0:T(8,128)(2,1)}, u32[]{:S(2)}) copy-start(bf16[32,4096]{1,0:T(8,128)(2,1)} %param.7) | copy-start | bytes 786436
Sparse Core Ops, SparseCore 0:
  16.7 79.5 all-gather.1

commit v8 on v5

--- a/solution.py
+++ b/solution.py
@@ -133,11 +133,15 @@
         out_rows.astype(jnp.bfloat16).reshape(tensor_size, -1, out_rows.shape[1]), "tensor", 0, 0, tiled=True
     )
     summed = jnp.sum(pieces.astype(jnp.float32), axis=0)
-    split_s = summed.reshape(summed.shape[0], 2, -1)
+    split_r = hidden_in.reshape(hidden_in.shape[0], -1, 2, 2, packed_rows)
+    split_r = jnp.transpose(split_r, (0, 3, 1, 2, 4)).reshape(hidden_in.shape[0], 2, -1)
+    split_r = lax.dynamic_slice_in_dim(jnp.concatenate((split_r, split_r), axis=1), core, 2, axis=1)
+    residual = split_r.reshape(hidden_in.shape).astype(jnp.float32)
+    hidden_perm = (summed + residual).astype(jnp.bfloat16)
+    split_s = hidden_perm.reshape(hidden_perm.shape[0], 2, -1)
     split_s = lax.dynamic_slice_in_dim(jnp.concatenate((split_s, split_s), axis=1), core, 2, axis=1)
-    split_s = split_s.reshape(summed.shape[0], 2, -1, 2, packed_rows)
-    summed = jnp.transpose(split_s, (0, 2, 3, 1, 4)).reshape(summed.shape)
-    hidden_out = (summed + rows_float).astype(jnp.bfloat16)
+    split_s = split_s.reshape(hidden_perm.shape[0], 2, -1, 2, packed_rows)
+    hidden_out = jnp.transpose(split_s, (0, 2, 3, 1, 4)).reshape(hidden_perm.shape)
     return (hidden_out, cache_rows)
 
 

time: 205 us -> 206 us (level)
  waiting for transfers between devices: 136 us -> 130 us
  local copies, waits for them, and re-layouts: 7.01 us -> 11.8 us
    all_to_all x1, waiting for transfers between devices: 26.4 us -> 21.3 us  [layer(): lax.all_to_all(out_rows.astype(jnp.bfloat16).reshape(tensor_size, -1, out...]
    reshape x3 -> x6, local copies, waits for them, and re-layouts: 2.15 us -> 6.76 us  [the longest x2 2.68 us: layer(): split_r = hidden_in.reshape(hidden_in.shape[0], -1, 2, 2, packed_rows)]
  transfers between devices with their start and end apart: 5 -> 5, of which waited for: 4 -> 4; matrix products, arithmetic and copies ran while one was open for 4% -> 6% of each run, Pallas kernels for 0% -> 0%
where the time goes in v8:
time: 206 us; the launch traced here: 205 us
  waiting for transfers between devices  130 us (63%)
  starting transfers between devices  24.4 us (12%)
  between operations  14.3 us (7%)
  other arithmetic  12.6 us (6%)
  local copies, waits for them, and re-layouts  11.8 us (6%)
  matrix products  11.1 us (5%)
    all_gather x1, waiting for transfers between devices, layer(): core_half = lax.all_gather(chip_pair, 'z', axis=0, tiled=True)  79.7 us
    all_to_all x1, waiting for transfers between devices, layer(): lax.all_to_all(jnp.broadcast_to(normed[None], (tensor_size,) + normed.sha...  26.8 us
    all_to_all x1, waiting for transfers between devices, layer(): lax.all_to_all(out_rows.astype(jnp.bfloat16).reshape(tensor_size, -1, out...  21.3 us
    ppermute x1, starting transfers between devices, layer(): other_half = lax.ppermute(core_half, 'c', [(0, 1), (1, 0)])  10.1 us
    all_to_all x1, starting transfers between devices, layer(): lax.all_to_all(jnp.broadcast_to(normed[None], (tensor_size,) + normed.sha...  6.42 us
  transfers between devices with their start and end apart: 5, of which 4 were waited for; matrix products, arithmetic and copies ran while one was open for 6% of the time, Pallas kernels for 0%

profile of v8, /device:TPU:1, one launch (start us, length us, event | category | flops | bytes accessed | tf_op | source)
XLA Modules:
  0.0 204.8 jit_solution(15524147126668675113)
XLA Ops:
  8.1 3.9 %collective-permute-start = (bf16[64,1280]{1,0:T(8,128)(2,1)S(1)}, bf16[64,1280]{1,0:T(8,128)(2,1)S(1)}, u32[]{:S(2)}, u32[]{:S(2)}) collective-permute-start(bf16[64,1280]{1,0:T(8,128)(2,1)S(1)} %pad_maximum_fusion.1), channel_id=1, source_target_pairs={{0,16},{16,0},{1,17},{17,1},{2,18},{18,2},{3,19},{19,3},{4,20},{20... | collective-permute-start | bytes 491528 | tf_op jit(solution)/shard_map/ppermute | solution.py:77
  12.1 2.7 %collective-permute-done = bf16[64,1280]{1,0:T(8,128)(2,1)S(1)} collective-permute-done((bf16[64,1280]{1,0:T(8,128)(2,1)S(1)}, bf16[64,1280]{1,0:T(8,128)(2,1)S(1)}, u32[]{:S(2)}, u32[]{:S(2)}) %collective-permute-start) | collective-permute-done | bytes 163872 | tf_op jit(solution)/shard_map/ppermute | solution.py:77
  14.8 1.8 maximum_select_fusion
  16.6 79.7 %all-gather.2.cloned.1.call-done = bf16[2048,1280]{1,0:T(8,128)(2,1)} async-done(((bf16[128,1280]{1,0:T(8,128)(2,1)}), bf16[2048,1280]{1,0:T(8,128)(2,1)}) %all-gather.2.cloned.1.call-update) | async-done | bytes 5242896 | tf_op jit(solution)/shard_map/all_gather | solution.py:82
  96.3 10.1 %collective-permute-start.1 = (bf16[2048,1280]{1,0:T(8,128)(2,1)}, bf16[2048,1280]{1,0:T(8,128)(2,1)}, u32[]{:S(2)}, u32[]{:S(2)}) collective-permute-start(bf16[2048,1280]{1,0:T(8,128)(2,1)} %all-gather.2.cloned.1.call-done), channel_id=1, source_target_pairs={{0,8},{8,0},{1,9},{9,1},{2,10},{10,2},{3,11},{11,3},{4,12},{12,4},... | collective-permute-start | bytes 15728648 | tf_op jit(solution)/shard_map/ppermute | solution.py:83
  107.1 1.1 fusion.15
  108.2 1.1 fusion.17
  110.8 1.5 broadcast_in_dim.16
  112.3 6.4 %all-to-all-start = ((bf16[8,32,4096]{2,1,0:T(8,128)(2,1)}), bf16[8,32,4096]{2,1,0:T(8,128)(2,1)S(1)}, u32[]{:S(2)}, u32[]{:S(2)}) async-start(bf16[8,32,4096]{2,1,0:T(8,128)(2,1)} %broadcast_in_dim.16), calls=%async_computation | async-start | bytes 4194304 | tf_op jit(solution)/shard_map/all_to_all | solution.py:73
  120.2 26.8 %all-to-all-done = bf16[8,32,4096]{2,1,0:T(8,128)(2,1)S(1)} async-done(((bf16[8,32,4096]{2,1,0:T(8,128)(2,1)}), bf16[8,32,4096]{2,1,0:T(8,128)(2,1)S(1)}, u32[]{:S(2)}, u32[]{:S(2)}) %all-to-all-start) | async-done | bytes 2097184 | tf_op jit(solution)/shard_map/all_to_all | solution.py:73
  147.0 2.9 %fusion = f32[256,768]{1,0:T(8,128)S(1)} fusion(bf16[2048,1280]{1,0:T(8,128)(2,1)} %collective-permute-done.1, bf16[256,4096]{1,0:T(8,128)(2,1)S(1)} %bitcast.93), kind=kOutput, calls=%fused_computation.1 | convolution fusion | flops 805306368 | bytes 4980736 | tf_op jit(solution)/shard_map/dot_general | solution.py:88
  149.8 2.9 %fusion.5 = f32[256,768]{1,0:T(8,128)S(1)} fusion(f32[256,768]{1,0:T(8,128)S(1)} %fusion, bf16[2048,1280]{1,0:T(8,128)(2,1)} %all-gather.2.cloned.1.call-done, bf16[256,4096]{1,0:T(8,128)(2,1)S(1)} %bitcast.94), kind=kOutput, calls=%fused_computation.12 | convolution fusion | flops 805502976 | bytes 5767168 | tf_op jit(solution)/shard_map/dot_general | solution.py:86
  155.3 2.3 %convolution_convert_fusion.1 = bf16[8,32,2048]{2,1,0:T(8,128)(2,1)S(1)} fusion(bf16[8,32,512]{2,1,0:T(8,128)(2,1)S(1)} %dot_general.24, bf16[2048,1280]{1,0:T(8,128)(2,1)} %all-gather.2.cloned.1.call-done), kind=kOutput, calls=%fused_computation.6 | convolution fusion | flops 537395200 | bytes 3407872 | tf_op jit(solution)/shard_map/dot_general | solution.py:127
  157.7 2.3 %convolution_convert_fusion = bf16[8,32,2048]{2,1,0:T(8,128)(2,1)S(1)} fusion(bf16[8,32,512]{2,1,0:T(8,128)(2,1)S(1)} %dot_general.24, bf16[2048,1280]{1,0:T(8,128)(2,1)} %collective-permute-done.1), kind=kOutput, calls=%fused_computation.5 | convolution fusion | flops 537395200 | bytes 3407872 | tf_op jit(solution)/shard_map/dot_general | solution.py:128
  160.0 1.6 pad_maximum_fusion
  161.6 3.9 %all-to-all-start.1 = ((bf16[8,32,4096]{2,1,0:T(8,128)(2,1)}), bf16[8,32,4096]{2,1,0:T(8,128)(2,1)S(1)}, u32[]{:S(2)}, u32[]{:S(2)}) async-start(bf16[8,32,4096]{2,1,0:T(8,128)(2,1)} %pad_maximum_fusion), calls=%async_computation.1 | async-start | bytes 4194304 | tf_op jit(solution)/shard_map/all_to_all | solution.py:132
  165.5 1.3 reshape.164
  166.8 1.3 copy.49
  168.2 1.2 reshape.165
  169.4 1.2 copy.22
  171.3 21.3 %all-to-all-done.1 = bf16[8,32,4096]{2,1,0:T(8,128)(2,1)S(1)} async-done(((bf16[8,32,4096]{2,1,0:T(8,128)(2,1)}), bf16[8,32,4096]{2,1,0:T(8,128)(2,1)S(1)}, u32[]{:S(2)}, u32[]{:S(2)}) %all-to-all-start.1) | async-done | bytes 2097184 | tf_op jit(solution)/shard_map/all_to_all | solution.py:132
  193.3 1.0 add_convert_fusion
  194.4 1.0 fusion.22
  196.8 1.2 reshape.167
  (46 shorter events, 9.9 us)
Async XLA Ops:
  7.2 89.1 %all-gather.2.cloned.1.call-start = ((), (), s32[]{:S(2)}) async-start(), calls=%async_computation.2 | async-start | bytes 5570560 | tf_op jit(solution)/shard_map/all_gather | solution.py:82
  8.1 6.6 %collective-permute-start = (bf16[64,1280]{1,0:T(8,128)(2,1)S(1)}, bf16[64,1280]{1,0:T(8,128)(2,1)S(1)}, u32[]{:S(2)}, u32[]{:S(2)}) collective-permute-start(bf16[64,1280]{1,0:T(8,128)(2,1)S(1)} %pad_maximum_fusion.1), channel_id=1, source_target_pairs={{0,16},{16,0},{1,17},{17,1},{2,18},{18,2},{3,19},{19,3},{4,20},{20... | collective-permute-start | bytes 491528 | tf_op jit(solution)/shard_map/ppermute | solution.py:77
  96.3 50.7 %collective-permute-start.1 = (bf16[2048,1280]{1,0:T(8,128)(2,1)}, bf16[2048,1280]{1,0:T(8,128)(2,1)}, u32[]{:S(2)}, u32[]{:S(2)}) collective-permute-start(bf16[2048,1280]{1,0:T(8,128)(2,1)} %all-gather.2.cloned.1.call-done), channel_id=1, source_target_pairs={{0,8},{8,0},{1,9},{9,1},{2,10},{10,2},{3,11},{11,3},{4,12},{12,4},... | collective-permute-start | bytes 15728648 | tf_op jit(solution)/shard_map/ppermute | solution.py:83
  110.8 8.0 %copy-start.1 = (s32[256]{0:T(256)S(1)}, s32[256]{0:T(256)}, u32[]{:S(2)}) copy-start(s32[256]{0:T(256)} %param.13) | copy-start | bytes 3076
  112.3 34.7 %all-to-all-start = ((bf16[8,32,4096]{2,1,0:T(8,128)(2,1)}), bf16[8,32,4096]{2,1,0:T(8,128)(2,1)S(1)}, u32[]{:S(2)}, u32[]{:S(2)}) async-start(bf16[8,32,4096]{2,1,0:T(8,128)(2,1)} %broadcast_in_dim.16), calls=%async_computation | async-start | bytes 4194304 | tf_op jit(solution)/shard_map/all_to_all | solution.py:73
  161.6 3.9 %copy-start = (bf16[32,4096]{1,0:T(8,128)(2,1)S(1)}, bf16[32,4096]{1,0:T(8,128)(2,1)}, u32[]{:S(2)}) copy-start(bf16[32,4096]{1,0:T(8,128)(2,1)} %param.7) | copy-start | bytes 786436
  161.6 31.0 %all-to-all-start.1 = ((bf16[8,32,4096]{2,1,0:T(8,128)(2,1)}), bf16[8,32,4096]{2,1,0:T(8,128)(2,1)S(1)}, u32[]{:S(2)}, u32[]{:S(2)}) async-start(bf16[8,32,4096]{2,1,0:T(8,128)(2,1)} %pad_maximum_fusion), calls=%async_computation.1 | async-start | bytes 4194304 | tf_op jit(solution)/shard_map/all_to_all | solution.py:132
Sparse Core Ops, SparseCore 0:
  16.7 79.5 all-gather.1

commit v9 on v5

--- a/solution.py
+++ b/solution.py
@@ -83,9 +83,11 @@
     other_half = lax.ppermute(core_half, "c", [(0, 1), (1, 0)])
     half_rows = core_half.shape[0]
     proj_cols = query_cols + 2 * kv_cols
-    projected = jnp.dot(
+    own_part = jnp.dot(
         gathered[:, :half_rows], core_half[:, :proj_cols], preferred_element_type=jnp.float32
-    ) + jnp.dot(
+    )
+    own_part = lax.optimization_barrier(own_part)
+    projected = own_part + jnp.dot(
         gathered[:, half_rows:], other_half[:, :proj_cols], preferred_element_type=jnp.float32
     )
     position = positions_of(segment)

time: 205 us -> 205 us (level)
  transfers between devices with their start and end apart: 5 -> 5, of which waited for: 4 -> 4; matrix products, arithmetic and copies ran while one was open for 4% -> 5% of each run, Pallas kernels for 0% -> 0%
where the time goes in v9:
time: 205 us; the launch traced here: 204 us
  waiting for transfers between devices  136 us (66%)
  starting transfers between devices  24.3 us (12%)
  between operations  14.3 us (7%)
  other arithmetic  12.2 us (6%)
  matrix products  11.1 us (5%)
  local copies, waits for them, and re-layouts  7.01 us (3%)
    all_gather x1, waiting for transfers between devices, layer(): core_half = lax.all_gather(chip_pair, 'z', axis=0, tiled=True)  79.7 us
    all_to_all x1, waiting for transfers between devices, layer(): lax.all_to_all(jnp.broadcast_to(normed[None], (tensor_size,) + normed.sha...  26.8 us
    all_to_all x1, waiting for transfers between devices, layer(): lax.all_to_all(out_rows.astype(jnp.bfloat16).reshape(tensor_size, -1, out...  26.4 us
    ppermute x1, starting transfers between devices, layer(): other_half = lax.ppermute(core_half, 'c', [(0, 1), (1, 0)])  10.1 us
    all_to_all x1, starting transfers between devices, layer(): lax.all_to_all(jnp.broadcast_to(normed[None], (tensor_size,) + normed.sha...  6.42 us
  transfers between devices with their start and end apart: 5, of which 4 were waited for; matrix products, arithmetic and copies ran while one was open for 5% of the time, Pallas kernels for 0%

profile of v9, /device:TPU:1, one launch (start us, length us, event | category | flops | bytes accessed | tf_op | source)
XLA Modules:
  0.0 204.5 jit_solution(17690286678451962641)
XLA Ops:
  7.2 0.9 pad_maximum_fusion.1
  8.1 3.9 %collective-permute-start = (bf16[64,1280]{1,0:T(8,128)(2,1)S(1)}, bf16[64,1280]{1,0:T(8,128)(2,1)S(1)}, u32[]{:S(2)}, u32[]{:S(2)}) collective-permute-start(bf16[64,1280]{1,0:T(8,128)(2,1)S(1)} %pad_maximum_fusion.1), channel_id=1, source_target_pairs={{0,16},{16,0},{1,17},{17,1},{2,18},{18,2},{3,19},{19,3},{4,20},{20... | collective-permute-start | bytes 491528 | tf_op jit(solution)/shard_map/ppermute | solution.py:77
  12.1 2.7 %collective-permute-done = bf16[64,1280]{1,0:T(8,128)(2,1)S(1)} collective-permute-done((bf16[64,1280]{1,0:T(8,128)(2,1)S(1)}, bf16[64,1280]{1,0:T(8,128)(2,1)S(1)}, u32[]{:S(2)}, u32[]{:S(2)}) %collective-permute-start) | collective-permute-done | bytes 163872 | tf_op jit(solution)/shard_map/ppermute | solution.py:77
  14.8 1.8 maximum_select_fusion
  16.6 79.7 %all-gather.2.cloned.1.call-done = bf16[2048,1280]{1,0:T(8,128)(2,1)} async-done(((bf16[128,1280]{1,0:T(8,128)(2,1)}), bf16[2048,1280]{1,0:T(8,128)(2,1)}) %all-gather.2.cloned.1.call-update) | async-done | bytes 5242896 | tf_op jit(solution)/shard_map/all_gather | solution.py:82
  96.3 10.1 %collective-permute-start.1 = (bf16[2048,1280]{1,0:T(8,128)(2,1)}, bf16[2048,1280]{1,0:T(8,128)(2,1)}, u32[]{:S(2)}, u32[]{:S(2)}) collective-permute-start(bf16[2048,1280]{1,0:T(8,128)(2,1)} %all-gather.2.cloned.1.call-done), channel_id=1, source_target_pairs={{0,8},{8,0},{1,9},{9,1},{2,10},{10,2},{3,11},{11,3},{4,12},{12,4},... | collective-permute-start | bytes 15728648 | tf_op jit(solution)/shard_map/ppermute | solution.py:83
  106.4 0.7 convert_element_type.61
  107.1 1.1 fusion.15
  108.2 1.1 fusion.17
  110.8 1.5 broadcast_in_dim.16
  112.3 6.4 %all-to-all-start = ((bf16[8,32,4096]{2,1,0:T(8,128)(2,1)}), bf16[8,32,4096]{2,1,0:T(8,128)(2,1)S(1)}, u32[]{:S(2)}, u32[]{:S(2)}) async-start(bf16[8,32,4096]{2,1,0:T(8,128)(2,1)} %broadcast_in_dim.16), calls=%async_computation | async-start | bytes 4194304 | tf_op jit(solution)/shard_map/all_to_all | solution.py:73
  120.2 26.8 %all-to-all-done = bf16[8,32,4096]{2,1,0:T(8,128)(2,1)S(1)} async-done(((bf16[8,32,4096]{2,1,0:T(8,128)(2,1)}), bf16[8,32,4096]{2,1,0:T(8,128)(2,1)S(1)}, u32[]{:S(2)}, u32[]{:S(2)}) %all-to-all-start) | async-done | bytes 2097184 | tf_op jit(solution)/shard_map/all_to_all | solution.py:73
  147.0 2.9 %fusion.2 = f32[256,768]{1,0:T(8,128)S(1)} fusion(bf16[2048,1280]{1,0:T(8,128)(2,1)} %all-gather.2.cloned.1.call-done, bf16[256,4096]{1,0:T(8,128)(2,1)S(1)} %bitcast.89), kind=kOutput, calls=%fused_computation.3 | convolution fusion | flops 805306368 | bytes 4980736 | tf_op jit(solution)/shard_map/dot_general | solution.py:86
  149.9 2.9 %fusion.5 = f32[256,768]{1,0:T(8,128)S(1)} fusion(f32[256,768]{1,0:T(8,128)S(1)} %fusion.2, bf16[2048,1280]{1,0:T(8,128)(2,1)} %collective-permute-done.1, bf16[256,4096]{1,0:T(8,128)(2,1)S(1)} %bitcast.90), kind=kOutput, calls=%fused_computation.12 | convolution fusion | flops 805502976 | bytes 5767168 | tf_op jit(solution)/shard_map/dot_general | solution.py:90
  155.3 2.3 %convolution_convert_fusion.1 = bf16[8,32,2048]{2,1,0:T(8,128)(2,1)S(1)} fusion(bf16[8,32,512]{2,1,0:T(8,128)(2,1)S(1)} %dot_general.24, bf16[2048,1280]{1,0:T(8,128)(2,1)} %all-gather.2.cloned.1.call-done), kind=kOutput, calls=%fused_computation.6 | convolution fusion | flops 537395200 | bytes 3407872 | tf_op jit(solution)/shard_map/dot_general | solution.py:129
  157.7 2.3 %convolution_convert_fusion = bf16[8,32,2048]{2,1,0:T(8,128)(2,1)S(1)} fusion(bf16[8,32,512]{2,1,0:T(8,128)(2,1)S(1)} %dot_general.24, bf16[2048,1280]{1,0:T(8,128)(2,1)} %collective-permute-done.1), kind=kOutput, calls=%fused_computation.5 | convolution fusion | flops 537395200 | bytes 3407872 | tf_op jit(solution)/shard_map/dot_general | solution.py:130
  160.0 1.6 pad_maximum_fusion
  161.6 3.8 %all-to-all-start.1 = ((bf16[8,32,4096]{2,1,0:T(8,128)(2,1)}), bf16[8,32,4096]{2,1,0:T(8,128)(2,1)S(1)}, u32[]{:S(2)}, u32[]{:S(2)}) async-start(bf16[8,32,4096]{2,1,0:T(8,128)(2,1)} %pad_maximum_fusion), calls=%async_computation.1 | async-start | bytes 4194304 | tf_op jit(solution)/shard_map/all_to_all | solution.py:134
  166.1 26.4 %all-to-all-done.1 = bf16[8,32,4096]{2,1,0:T(8,128)(2,1)S(1)} async-done(((bf16[8,32,4096]{2,1,0:T(8,128)(2,1)}), bf16[8,32,4096]{2,1,0:T(8,128)(2,1)S(1)}, u32[]{:S(2)}, u32[]{:S(2)}) %all-to-all-start.1) | async-done | bytes 2097184 | tf_op jit(solution)/shard_map/all_to_all | solution.py:134
  193.2 0.8 fusion.21
  194.3 0.8 reshape.159
  195.1 0.8 copy.21
  195.9 0.9 reshape.160
  196.9 0.8 fusion.18
  (42 shorter events, 7.2 us)
Async XLA Ops:
  7.2 89.1 %all-gather.2.cloned.1.call-start = ((), (), s32[]{:S(2)}) async-start(), calls=%async_computation.2 | async-start | bytes 5570560 | tf_op jit(solution)/shard_map/all_gather | solution.py:82
  8.1 6.6 %collective-permute-start = (bf16[64,1280]{1,0:T(8,128)(2,1)S(1)}, bf16[64,1280]{1,0:T(8,128)(2,1)S(1)}, u32[]{:S(2)}, u32[]{:S(2)}) collective-permute-start(bf16[64,1280]{1,0:T(8,128)(2,1)S(1)} %pad_maximum_fusion.1), channel_id=1, source_target_pairs={{0,16},{16,0},{1,17},{17,1},{2,18},{18,2},{3,19},{19,3},{4,20},{20... | collective-permute-start | bytes 491528 | tf_op jit(solution)/shard_map/ppermute | solution.py:77
  96.3 53.5 %collective-permute-start.1 = (bf16[2048,1280]{1,0:T(8,128)(2,1)}, bf16[2048,1280]{1,0:T(8,128)(2,1)}, u32[]{:S(2)}, u32[]{:S(2)}) collective-permute-start(bf16[2048,1280]{1,0:T(8,128)(2,1)} %all-gather.2.cloned.1.call-done), channel_id=1, source_target_pairs={{0,8},{8,0},{1,9},{9,1},{2,10},{10,2},{3,11},{11,3},{4,12},{12,4},... | collective-permute-start | bytes 15728648 | tf_op jit(solution)/shard_map/ppermute | solution.py:83
  110.8 8.0 %copy-start.1 = (s32[256]{0:T(256)S(1)}, s32[256]{0:T(256)}, u32[]{:S(2)}) copy-start(s32[256]{0:T(256)} %param.13) | copy-start | bytes 3076
  112.3 34.7 %all-to-all-start = ((bf16[8,32,4096]{2,1,0:T(8,128)(2,1)}), bf16[8,32,4096]{2,1,0:T(8,128)(2,1)S(1)}, u32[]{:S(2)}, u32[]{:S(2)}) async-start(bf16[8,32,4096]{2,1,0:T(8,128)(2,1)} %broadcast_in_dim.16), calls=%async_computation | async-start | bytes 4194304 | tf_op jit(solution)/shard_map/all_to_all | solution.py:73
  161.6 30.9 %all-to-all-start.1 = ((bf16[8,32,4096]{2,1,0:T(8,128)(2,1)}), bf16[8,32,4096]{2,1,0:T(8,128)(2,1)S(1)}, u32[]{:S(2)}, u32[]{:S(2)}) async-start(bf16[8,32,4096]{2,1,0:T(8,128)(2,1)} %pad_maximum_fusion), calls=%async_computation.1 | async-start | bytes 4194304 | tf_op jit(solution)/shard_map/all_to_all | solution.py:134
  194.0 2.9 %copy-start = (bf16[32,4096]{1,0:T(8,128)(2,1)S(1)}, bf16[32,4096]{1,0:T(8,128)(2,1)}, u32[]{:S(2)}) copy-start(bf16[32,4096]{1,0:T(8,128)(2,1)} %param.7) | copy-start | bytes 786436
Sparse Core Ops, SparseCore 0:
  16.7 79.5 all-gather.1

commit v10 on v8

--- a/solution.py
+++ b/solution.py
@@ -83,9 +83,11 @@
     other_half = lax.ppermute(core_half, "c", [(0, 1), (1, 0)])
     half_rows = core_half.shape[0]
     proj_cols = query_cols + 2 * kv_cols
-    projected = jnp.dot(
+    own_part = jnp.dot(
         gathered[:, :half_rows], core_half[:, :proj_cols], preferred_element_type=jnp.float32
-    ) + jnp.dot(
+    )
+    own_part = lax.optimization_barrier(own_part)
+    projected = own_part + jnp.dot(
         gathered[:, half_rows:], other_half[:, :proj_cols], preferred_element_type=jnp.float32
     )
     position = positions_of(segment)

time: 206 us -> 206 us (level)
  transfers between devices with their start and end apart: 5 -> 5, of which waited for: 4 -> 4; matrix products, arithmetic and copies ran while one was open for 6% -> 8% of each run, Pallas kernels for 0% -> 0%
where the time goes in v10:
time: 206 us; the launch traced here: 205 us
  waiting for transfers between devices  130 us (63%)
  starting transfers between devices  24.4 us (12%)
  between operations  14.3 us (7%)
  other arithmetic  12.6 us (6%)
  local copies, waits for them, and re-layouts  11.8 us (6%)
  matrix products  11.1 us (5%)
    all_gather x1, waiting for transfers between devices, layer(): core_half = lax.all_gather(chip_pair, 'z', axis=0, tiled=True)  79.7 us
    all_to_all x1, waiting for transfers between devices, layer(): lax.all_to_all(jnp.broadcast_to(normed[None], (tensor_size,) + normed.sha...  26.8 us
    all_to_all x1, waiting for transfers between devices, layer(): lax.all_to_all(out_rows.astype(jnp.bfloat16).reshape(tensor_size, -1, out...  21.3 us
    ppermute x1, starting transfers between devices, layer(): other_half = lax.ppermute(core_half, 'c', [(0, 1), (1, 0)])  10.1 us
    all_to_all x1, starting transfers between devices, layer(): lax.all_to_all(jnp.broadcast_to(normed[None], (tensor_size,) + normed.sha...  6.42 us
  transfers between devices with their start and end apart: 5, of which 4 were waited for; matrix products, arithmetic and copies ran while one was open for 8% of the time, Pallas kernels for 0%

profile of v10, /device:TPU:1, one launch (start us, length us, event | category | flops | bytes accessed | tf_op | source)
XLA Modules:
  0.0 204.8 jit_solution(12635979098593139554)
XLA Ops:
  8.1 3.9 %collective-permute-start = (bf16[64,1280]{1,0:T(8,128)(2,1)S(1)}, bf16[64,1280]{1,0:T(8,128)(2,1)S(1)}, u32[]{:S(2)}, u32[]{:S(2)}) collective-permute-start(bf16[64,1280]{1,0:T(8,128)(2,1)S(1)} %pad_maximum_fusion.1), channel_id=1, source_target_pairs={{0,16},{16,0},{1,17},{17,1},{2,18},{18,2},{3,19},{19,3},{4,20},{20... | collective-permute-start | bytes 491528 | tf_op jit(solution)/shard_map/ppermute | solution.py:77
  12.1 2.7 %collective-permute-done = bf16[64,1280]{1,0:T(8,128)(2,1)S(1)} collective-permute-done((bf16[64,1280]{1,0:T(8,128)(2,1)S(1)}, bf16[64,1280]{1,0:T(8,128)(2,1)S(1)}, u32[]{:S(2)}, u32[]{:S(2)}) %collective-permute-start) | collective-permute-done | bytes 163872 | tf_op jit(solution)/shard_map/ppermute | solution.py:77
  14.8 1.8 maximum_select_fusion
  16.6 79.7 %all-gather.2.cloned.1.call-done = bf16[2048,1280]{1,0:T(8,128)(2,1)} async-done(((bf16[128,1280]{1,0:T(8,128)(2,1)}), bf16[2048,1280]{1,0:T(8,128)(2,1)}) %all-gather.2.cloned.1.call-update) | async-done | bytes 5242896 | tf_op jit(solution)/shard_map/all_gather | solution.py:82
  96.3 10.1 %collective-permute-start.1 = (bf16[2048,1280]{1,0:T(8,128)(2,1)}, bf16[2048,1280]{1,0:T(8,128)(2,1)}, u32[]{:S(2)}, u32[]{:S(2)}) collective-permute-start(bf16[2048,1280]{1,0:T(8,128)(2,1)} %all-gather.2.cloned.1.call-done), channel_id=1, source_target_pairs={{0,8},{8,0},{1,9},{9,1},{2,10},{10,2},{3,11},{11,3},{4,12},{12,4},... | collective-permute-start | bytes 15728648 | tf_op jit(solution)/shard_map/ppermute | solution.py:83
  107.1 1.1 fusion.15
  108.2 1.1 fusion.17
  110.8 1.5 broadcast_in_dim.16
  112.3 6.4 %all-to-all-start = ((bf16[8,32,4096]{2,1,0:T(8,128)(2,1)}), bf16[8,32,4096]{2,1,0:T(8,128)(2,1)S(1)}, u32[]{:S(2)}, u32[]{:S(2)}) async-start(bf16[8,32,4096]{2,1,0:T(8,128)(2,1)} %broadcast_in_dim.16), calls=%async_computation | async-start | bytes 4194304 | tf_op jit(solution)/shard_map/all_to_all | solution.py:73
  120.2 26.8 %all-to-all-done = bf16[8,32,4096]{2,1,0:T(8,128)(2,1)S(1)} async-done(((bf16[8,32,4096]{2,1,0:T(8,128)(2,1)}), bf16[8,32,4096]{2,1,0:T(8,128)(2,1)S(1)}, u32[]{:S(2)}, u32[]{:S(2)}) %all-to-all-start) | async-done | bytes 2097184 | tf_op jit(solution)/shard_map/all_to_all | solution.py:73
  147.0 2.9 %fusion.2 = f32[256,768]{1,0:T(8,128)S(1)} fusion(bf16[2048,1280]{1,0:T(8,128)(2,1)} %all-gather.2.cloned.1.call-done, bf16[256,4096]{1,0:T(8,128)(2,1)S(1)} %bitcast.93), kind=kOutput, calls=%fused_computation.3 | convolution fusion | flops 805306368 | bytes 4980736 | tf_op jit(solution)/shard_map/dot_general | solution.py:86
  149.9 2.9 %fusion.5 = f32[256,768]{1,0:T(8,128)S(1)} fusion(f32[256,768]{1,0:T(8,128)S(1)} %fusion.2, bf16[2048,1280]{1,0:T(8,128)(2,1)} %collective-permute-done.1, bf16[256,4096]{1,0:T(8,128)(2,1)S(1)} %bitcast.94), kind=kOutput, calls=%fused_computation.12 | convolution fusion | flops 805502976 | bytes 5767168 | tf_op jit(solution)/shard_map/dot_general | solution.py:90
  155.3 2.3 %convolution_convert_fusion.1 = bf16[8,32,2048]{2,1,0:T(8,128)(2,1)S(1)} fusion(bf16[8,32,512]{2,1,0:T(8,128)(2,1)S(1)} %dot_general.24, bf16[2048,1280]{1,0:T(8,128)(2,1)} %all-gather.2.cloned.1.call-done), kind=kOutput, calls=%fused_computation.6 | convolution fusion | flops 537395200 | bytes 3407872 | tf_op jit(solution)/shard_map/dot_general | solution.py:129
  157.7 2.3 %convolution_convert_fusion = bf16[8,32,2048]{2,1,0:T(8,128)(2,1)S(1)} fusion(bf16[8,32,512]{2,1,0:T(8,128)(2,1)S(1)} %dot_general.24, bf16[2048,1280]{1,0:T(8,128)(2,1)} %collective-permute-done.1), kind=kOutput, calls=%fused_computation.5 | convolution fusion | flops 537395200 | bytes 3407872 | tf_op jit(solution)/shard_map/dot_general | solution.py:130
  160.0 1.6 pad_maximum_fusion
  161.6 3.9 %all-to-all-start.1 = ((bf16[8,32,4096]{2,1,0:T(8,128)(2,1)}), bf16[8,32,4096]{2,1,0:T(8,128)(2,1)S(1)}, u32[]{:S(2)}, u32[]{:S(2)}) async-start(bf16[8,32,4096]{2,1,0:T(8,128)(2,1)} %pad_maximum_fusion), calls=%async_computation.1 | async-start | bytes 4194304 | tf_op jit(solution)/shard_map/all_to_all | solution.py:134
  165.5 1.3 reshape.164
  166.9 1.3 copy.49
  168.2 1.2 reshape.165
  169.4 1.2 copy.22
  171.3 21.3 %all-to-all-done.1 = bf16[8,32,4096]{2,1,0:T(8,128)(2,1)S(1)} async-done(((bf16[8,32,4096]{2,1,0:T(8,128)(2,1)}), bf16[8,32,4096]{2,1,0:T(8,128)(2,1)S(1)}, u32[]{:S(2)}, u32[]{:S(2)}) %all-to-all-start.1) | async-done | bytes 2097184 | tf_op jit(solution)/shard_map/all_to_all | solution.py:134
  193.3 1.0 add_convert_fusion
  194.4 1.0 fusion.22
  196.8 1.2 reshape.167
  (46 shorter events, 9.9 us)
Async XLA Ops:
  7.2 89.1 %all-gather.2.cloned.1.call-start = ((), (), s32[]{:S(2)}) async-start(), calls=%async_computation.2 | async-start | bytes 5570560 | tf_op jit(solution)/shard_map/all_gather | solution.py:82
  8.1 6.6 %collective-permute-start = (bf16[64,1280]{1,0:T(8,128)(2,1)S(1)}, bf16[64,1280]{1,0:T(8,128)(2,1)S(1)}, u32[]{:S(2)}, u32[]{:S(2)}) collective-permute-start(bf16[64,1280]{1,0:T(8,128)(2,1)S(1)} %pad_maximum_fusion.1), channel_id=1, source_target_pairs={{0,16},{16,0},{1,17},{17,1},{2,18},{18,2},{3,19},{19,3},{4,20},{20... | collective-permute-start | bytes 491528 | tf_op jit(solution)/shard_map/ppermute | solution.py:77
  96.3 53.5 %collective-permute-start.1 = (bf16[2048,1280]{1,0:T(8,128)(2,1)}, bf16[2048,1280]{1,0:T(8,128)(2,1)}, u32[]{:S(2)}, u32[]{:S(2)}) collective-permute-start(bf16[2048,1280]{1,0:T(8,128)(2,1)} %all-gather.2.cloned.1.call-done), channel_id=1, source_target_pairs={{0,8},{8,0},{1,9},{9,1},{2,10},{10,2},{3,11},{11,3},{4,12},{12,4},... | collective-permute-start | bytes 15728648 | tf_op jit(solution)/shard_map/ppermute | solution.py:83
  110.8 8.0 %copy-start.1 = (s32[256]{0:T(256)S(1)}, s32[256]{0:T(256)}, u32[]{:S(2)}) copy-start(s32[256]{0:T(256)} %param.13) | copy-start | bytes 3076
  112.3 34.7 %all-to-all-start = ((bf16[8,32,4096]{2,1,0:T(8,128)(2,1)}), bf16[8,32,4096]{2,1,0:T(8,128)(2,1)S(1)}, u32[]{:S(2)}, u32[]{:S(2)}) async-start(bf16[8,32,4096]{2,1,0:T(8,128)(2,1)} %broadcast_in_dim.16), calls=%async_computation | async-start | bytes 4194304 | tf_op jit(solution)/shard_map/all_to_all | solution.py:73
  161.6 3.9 %copy-start = (bf16[32,4096]{1,0:T(8,128)(2,1)S(1)}, bf16[32,4096]{1,0:T(8,128)(2,1)}, u32[]{:S(2)}) copy-start(bf16[32,4096]{1,0:T(8,128)(2,1)} %param.7) | copy-start | bytes 786436
  161.6 31.0 %all-to-all-start.1 = ((bf16[8,32,4096]{2,1,0:T(8,128)(2,1)}), bf16[8,32,4096]{2,1,0:T(8,128)(2,1)S(1)}, u32[]{:S(2)}, u32[]{:S(2)}) async-start(bf16[8,32,4096]{2,1,0:T(8,128)(2,1)} %pad_maximum_fusion), calls=%async_computation.1 | async-start | bytes 4194304 | tf_op jit(solution)/shard_map/all_to_all | solution.py:134
Sparse Core Ops, SparseCore 0:
  16.7 79.5 all-gather.1

commit v11 on v9

--- a/solution.py
+++ b/solution.py
@@ -80,15 +80,16 @@
         first_xl, jnp.concatenate((packed, pair)), jnp.concatenate((pair, packed))
     )
     core_half = lax.all_gather(chip_pair, "z", axis=0, tiled=True)
-    other_half = lax.ppermute(core_half, "c", [(0, 1), (1, 0)])
+    proj_cols = query_cols + 2 * kv_cols
+    other_proj = lax.ppermute(core_half[:, :proj_cols], "c", [(0, 1), (1, 0)])
+    other_out = lax.ppermute(core_half[:, proj_cols:], "c", [(0, 1), (1, 0)])
     half_rows = core_half.shape[0]
-    proj_cols = query_cols + 2 * kv_cols
     own_part = jnp.dot(
         gathered[:, :half_rows], core_half[:, :proj_cols], preferred_element_type=jnp.float32
     )
     own_part = lax.optimization_barrier(own_part)
     projected = own_part + jnp.dot(
-        gathered[:, half_rows:], other_half[:, :proj_cols], preferred_element_type=jnp.float32
+        gathered[:, half_rows:], other_proj, preferred_element_type=jnp.float32
     )
     position = positions_of(segment)
     query_rows = rotate(
@@ -127,7 +128,7 @@
     out_rows = jnp.concatenate(
         (
             lax.dot_general(attended, core_half[:, proj_cols:], out_dims, preferred_element_type=jnp.float32),
-            lax.dot_general(attended, other_half[:, proj_cols:], out_dims, preferred_element_type=jnp.float32),
+            lax.dot_general(attended, other_out, out_dims, preferred_element_type=jnp.float32),
         ),
         axis=1,
     )

time: 205 us -> 220 us (1.073)
  local copies, waits for them, and re-layouts: 7.01 us -> 18.1 us
  starting transfers between devices: 24.3 us -> 27.5 us
    slice x1 -> x3, local copies, waits for them, and re-layouts: 0.07 us -> 5.19 us  [the longest x1 3.02 us: layer(): core_half[:, proj_cols:]]
    reshape x2, local copies, waits for them, and re-layouts: 0.84 us -> 4.54 us  [layer(): split_d = normed.reshape(normed.shape[0], -1, 2, 2, packed_rows)]
    ppermute x1 -> x2, starting transfers between devices: 10.1 us -> 13.2 us  [the longest x1 10.1 us: layer(): other_proj = lax.ppermute(core_half[:, :proj_cols], 'c', [(0, 1), (1, 0)])]
  transfers between devices with their start and end apart: 5 -> 6, of which waited for: 4 -> 4; matrix products, arithmetic and copies ran while one was open for 5% -> 14% of each run, Pallas kernels for 0% -> 0%
where the time goes in v11:
time: 220 us
  waiting for transfers between devices  134 us (61%)
  starting transfers between devices  27.5 us (12%)
  local copies, waits for them, and re-layouts  18.1 us (8%)
  between operations  14.3 us (6%)
  other arithmetic  14.1 us (6%)
  matrix products  11.8 us (5%)
    all_gather x1, waiting for transfers between devices, layer(): core_half = lax.all_gather(chip_pair, 'z', axis=0, tiled=True)  77.9 us
    all_to_all x1, waiting for transfers between devices, layer(): lax.all_to_all(out_rows.astype(jnp.bfloat16).reshape(tensor_size, -1, out...  27.6 us
    all_to_all x1, waiting for transfers between devices, layer(): lax.all_to_all(jnp.broadcast_to(normed[None], (tensor_size,) + normed.sha...  25.6 us
    ppermute x1, starting transfers between devices, layer(): other_proj = lax.ppermute(core_half[:, :proj_cols], 'c', [(0, 1), (1, 0)])  10.1 us
    all_to_all x1, starting transfers between devices, layer(): lax.all_to_all(jnp.broadcast_to(normed[None], (tensor_size,) + normed.sha...  6.55 us
    reshape x2, local copies, waits for them, and re-layouts, layer(): split_d = normed.reshape(normed.shape[0], -1, 2, 2, packed_rows)  4.54 us
  transfers between devices with their start and end apart: 6, of which 4 were waited for; matrix products, arithmetic and copies ran while one was open for 14% of the time, Pallas kernels for 0%

profile of v11, /device:TPU:1, one launch (start us, length us, event | category | flops | bytes accessed | tf_op | source)
XLA Modules:
  0.0 219.6 jit_solution(17495658024040559573)
XLA Ops:
  8.1 3.9 %collective-permute-start = (bf16[64,1280]{1,0:T(8,128)(2,1)S(1)}, bf16[64,1280]{1,0:T(8,128)(2,1)S(1)}, u32[]{:S(2)}, u32[]{:S(2)}) collective-permute-start(bf16[64,1280]{1,0:T(8,128)(2,1)S(1)} %pad_maximum_fusion.1), channel_id=1, source_target_pairs={{0,16},{16,0},{1,17},{17,1},{2,18},{18,2},{3,19},{19,3},{4,20},{20... | collective-permute-start | bytes 491528 | tf_op jit(solution)/shard_map/ppermute | solution.py:77
  12.1 2.7 %collective-permute-done = bf16[64,1280]{1,0:T(8,128)(2,1)S(1)} collective-permute-done((bf16[64,1280]{1,0:T(8,128)(2,1)S(1)}, bf16[64,1280]{1,0:T(8,128)(2,1)S(1)}, u32[]{:S(2)}, u32[]{:S(2)}) %collective-permute-start) | collective-permute-done | bytes 163872 | tf_op jit(solution)/shard_map/ppermute | solution.py:77
  14.8 1.8 maximum_select_fusion
  17.3 1.1 fusion.11
  18.4 77.9 %all-gather.2.cloned.1.call-done = bf16[2048,1280]{1,0:T(8,128)(2,1)} async-done(((bf16[128,1280]{1,0:T(8,128)(2,1)}), bf16[2048,1280]{1,0:T(8,128)(2,1)}) %all-gather.2.cloned.1.call-update) | async-done | bytes 5242896 | tf_op jit(solution)/shard_map/all_gather | solution.py:82
  96.3 2.1 slice.65
  98.4 10.1 %collective-permute-start.1 = (bf16[2048,768]{1,0:T(8,128)(2,1)S(1)}, bf16[2048,768]{1,0:T(8,128)(2,1)}, u32[]{:S(2)}, u32[]{:S(2)}) collective-permute-start(bf16[2048,768]{1,0:T(8,128)(2,1)S(1)} %slice.65), channel_id=1, source_target_pairs={{0,8},{8,0},{1,9},{9,1},{2,10},{10,2},{3,11},{11,3},{4,12},{12,4},... | collective-permute-start | bytes 9437192 | tf_op jit(solution)/shard_map/ppermute | solution.py:84
  109.3 2.3 %reshape.151 = bf16[32,16,2,2,64]{4,3,2,1,0:T(2,128)(2,1)} reshape(bf16[32,4096]{1,0:T(8,128)(2,1)} %fusion.13) | data formatting | bytes 524288 | tf_op jit(solution)/shard_map/reshape | solution.py:69
  111.7 2.2 %copy.44 = bf16[32,16,2,2,64]{4,2,1,0,3:T(2,128)(2,1)} copy(bf16[32,16,2,2,64]{4,3,2,1,0:T(2,128)(2,1)} %reshape.151) | data formatting | bytes 524288 | tf_op jit(solution)/shard_map/reshape | solution.py:69
  113.9 2.2 %reshape.152 = bf16[32,2,2048]{2,0,1:T(8,128)(2,1)} reshape(bf16[32,2,16,2,64]{4,3,2,0,1:T(2,128)(2,1)} %bitcast.91) | data formatting | bytes 524288 | tf_op jit(solution)/shard_map/reshape | solution.py:70
  116.1 1.1 fusion.21
  117.2 1.5 broadcast_in_dim.16
  118.7 6.6 %all-to-all-start = ((bf16[8,32,4096]{2,1,0:T(8,128)(2,1)}), bf16[8,32,4096]{2,1,0:T(8,128)(2,1)}, u32[]{:S(2)}, u32[]{:S(2)}) async-start(bf16[8,32,4096]{2,1,0:T(8,128)(2,1)} %broadcast_in_dim.16), calls=%async_computation | async-start | bytes 4194304 | tf_op jit(solution)/shard_map/all_to_all | solution.py:73
  126.8 1.2 multiply_cosine_fusion
  128.0 25.6 %all-to-all-done = bf16[8,32,4096]{2,1,0:T(8,128)(2,1)} async-done(((bf16[8,32,4096]{2,1,0:T(8,128)(2,1)}), bf16[8,32,4096]{2,1,0:T(8,128)(2,1)}, u32[]{:S(2)}, u32[]{:S(2)}) %all-to-all-start) | async-done | bytes 2097184 | tf_op jit(solution)/shard_map/all_to_all | solution.py:73
  153.6 3.2 %fusion.7 = f32[256,768]{1,0:T(8,128)S(1)} fusion(bf16[256,4096]{1,0:T(8,128)(2,1)} %bitcast.1, bf16[2048,1280]{1,0:T(8,128)(2,1)} %all-gather.2.cloned.1.call-done), kind=kOutput, calls=%fused_computation.14 | convolution fusion | flops 805306368 | bytes 4980736 | tf_op jit(solution)/shard_map/dot_general | solution.py:87
  156.8 3.0 %slice.74 = bf16[2048,512]{1,0:T(8,128)(2,1)} slice(bf16[2048,1280]{1,0:T(8,128)(2,1)} %all-gather.2.cloned.1.call-done), slice={[0:2048], [768:1280]} | slice | bytes 4194304 | tf_op jit(solution)/shard_map/slice | solution.py:130
  159.8 3.1 %collective-permute-start.2 = (bf16[2048,512]{1,0:T(8,128)(2,1)}, bf16[2048,512]{1,0:T(8,128)(2,1)}, u32[]{:S(2)}, u32[]{:S(2)}) collective-permute-start(bf16[2048,512]{1,0:T(8,128)(2,1)} %slice.74), channel_id=1, source_target_pairs={{0,8},{8,0},{1,9},{9,1},{2,10},{10,2},{3,11},{11,3},{4,12},{12,4},... | collective-permute-start | bytes 6291464 | tf_op jit(solution)/shard_map/ppermute | solution.py:85
  162.9 3.2 %convolution_add_fusion = f32[256,768]{1,0:T(8,128)S(1)} fusion(f32[256,768]{1,0:T(8,128)S(1)} %fusion.7, bf16[2048,768]{1,0:T(8,128)(2,1)} %collective-permute-done.1, bf16[256,4096]{1,0:T(8,128)(2,1)} %bitcast.1), kind=kOutput, calls=%fused_computation.8 | convolution fusion | flops 805502976 | bytes 5767168 | tf_op jit(solution)/shard_map/dot_general | solution.py:91
  169.3 2.3 %convolution_convert_fusion.1 = bf16[8,32,2048]{2,1,0:T(8,128)(2,1)S(1)} fusion(bf16[8,32,512]{2,1,0:T(8,128)(2,1)S(1)} %dot_general.24, bf16[2048,1280]{1,0:T(8,128)(2,1)} %all-gather.2.cloned.1.call-done), kind=kOutput, calls=%fused_computation.2 | convolution fusion | flops 537395200 | bytes 3407872 | tf_op jit(solution)/shard_map/dot_general | solution.py:130
  171.6 2.3 %convolution_convert_fusion = bf16[8,32,2048]{2,1,0:T(8,128)(2,1)S(1)} fusion(bf16[8,32,512]{2,1,0:T(8,128)(2,1)S(1)} %dot_general.24, bf16[2048,512]{1,0:T(8,128)(2,1)} %collective-permute-done.2), kind=kOutput, calls=%fused_computation.1 | convolution fusion | flops 537395200 | bytes 3407872 | tf_op jit(solution)/shard_map/dot_general | solution.py:131
  174.0 1.6 pad_maximum_fusion
  175.6 3.8 %all-to-all-start.1 = ((bf16[8,32,4096]{2,1,0:T(8,128)(2,1)}), bf16[8,32,4096]{2,1,0:T(8,128)(2,1)S(1)}, u32[]{:S(2)}, u32[]{:S(2)}) async-start(bf16[8,32,4096]{2,1,0:T(8,128)(2,1)} %pad_maximum_fusion), calls=%async_computation.1 | async-start | bytes 4194304 | tf_op jit(solution)/shard_map/all_to_all | solution.py:135
  180.0 27.6 %all-to-all-done.1 = bf16[8,32,4096]{2,1,0:T(8,128)(2,1)S(1)} async-done(((bf16[8,32,4096]{2,1,0:T(8,128)(2,1)}), bf16[8,32,4096]{2,1,0:T(8,128)(2,1)S(1)}, u32[]{:S(2)}, u32[]{:S(2)}) %all-to-all-start.1) | async-done | bytes 2097184 | tf_op jit(solution)/shard_map/all_to_all | solution.py:135
  (50 shorter events, 12.9 us)
Async XLA Ops:
  7.2 89.1 %all-gather.2.cloned.1.call-start = ((), (), s32[]{:S(2)}) async-start(), calls=%async_computation.2 | async-start | bytes 5570560 | tf_op jit(solution)/shard_map/all_gather | solution.py:82
  8.1 6.6 %collective-permute-start = (bf16[64,1280]{1,0:T(8,128)(2,1)S(1)}, bf16[64,1280]{1,0:T(8,128)(2,1)S(1)}, u32[]{:S(2)}, u32[]{:S(2)}) collective-permute-start(bf16[64,1280]{1,0:T(8,128)(2,1)S(1)} %pad_maximum_fusion.1), channel_id=1, source_target_pairs={{0,16},{16,0},{1,17},{17,1},{2,18},{18,2},{3,19},{19,3},{4,20},{20... | collective-permute-start | bytes 491528 | tf_op jit(solution)/shard_map/ppermute | solution.py:77
  18.4 90.1 %copy-start = (bf16[32,4096]{1,0:T(8,128)(2,1)S(1)}, bf16[32,4096]{1,0:T(8,128)(2,1)}, u32[]{:S(2)}) copy-start(bf16[32,4096]{1,0:T(8,128)(2,1)} %param.7) | copy-start | bytes 786436
  98.4 64.5 %collective-permute-start.1 = (bf16[2048,768]{1,0:T(8,128)(2,1)S(1)}, bf16[2048,768]{1,0:T(8,128)(2,1)}, u32[]{:S(2)}, u32[]{:S(2)}) collective-permute-start(bf16[2048,768]{1,0:T(8,128)(2,1)S(1)} %slice.65), channel_id=1, source_target_pairs={{0,8},{8,0},{1,9},{9,1},{2,10},{10,2},{3,11},{11,3},{4,12},{12,4},... | collective-permute-start | bytes 9437192 | tf_op jit(solution)/shard_map/ppermute | solution.py:84
  118.7 6.6 %copy-start.3 = (s32[256]{0:T(256)S(1)}, s32[256]{0:T(256)}, u32[]{:S(2)}) copy-start(s32[256]{0:T(256)} %param.13) | copy-start | bytes 3076
  118.7 34.9 %all-to-all-start = ((bf16[8,32,4096]{2,1,0:T(8,128)(2,1)}), bf16[8,32,4096]{2,1,0:T(8,128)(2,1)}, u32[]{:S(2)}, u32[]{:S(2)}) async-start(bf16[8,32,4096]{2,1,0:T(8,128)(2,1)} %broadcast_in_dim.16), calls=%async_computation | async-start | bytes 4194304 | tf_op jit(solution)/shard_map/all_to_all | solution.py:73
  159.8 11.8 %collective-permute-start.2 = (bf16[2048,512]{1,0:T(8,128)(2,1)}, bf16[2048,512]{1,0:T(8,128)(2,1)}, u32[]{:S(2)}, u32[]{:S(2)}) collective-permute-start(bf16[2048,512]{1,0:T(8,128)(2,1)} %slice.74), channel_id=1, source_target_pairs={{0,8},{8,0},{1,9},{9,1},{2,10},{10,2},{3,11},{11,3},{4,12},{12,4},... | collective-permute-start | bytes 6291464 | tf_op jit(solution)/shard_map/ppermute | solution.py:85
  166.1 0.9 copy-start.1
  167.2 0.8 copy-start.2
  175.6 32.1 %all-to-all-start.1 = ((bf16[8,32,4096]{2,1,0:T(8,128)(2,1)}), bf16[8,32,4096]{2,1,0:T(8,128)(2,1)S(1)}, u32[]{:S(2)}, u32[]{:S(2)}) async-start(bf16[8,32,4096]{2,1,0:T(8,128)(2,1)} %pad_maximum_fusion), calls=%async_computation.1 | async-start | bytes 4194304 | tf_op jit(solution)/shard_map/all_to_all | solution.py:135
Sparse Core Ops, SparseCore 0:
  16.7 79.5 all-gather.1

commit v12 on v6

--- a/solution.py
+++ b/solution.py
@@ -75,16 +75,20 @@
     gathered = lax.all_to_all(
         jnp.broadcast_to(normed[None], (tensor_size,) + normed.shape), "tensor", 0, 0, tiled=True
     ).reshape(pack_rows, normed.shape[1])
-    packed = jnp.concatenate((w_query, w_key, w_value, w_out.T), axis=1)
-    pair = lax.ppermute(packed, "xl", [(0, 1), (1, 0)])
-    chip_pair = jnp.concatenate((packed, pair))
+    shards = (w_query, w_key, w_value, w_out.T)
+    pairs = tuple(lax.ppermute(w, "xl", [(0, 1), (1, 0)]) for w in shards)
+    chip_pair = jnp.concatenate(
+        (jnp.concatenate(shards, axis=1), jnp.concatenate(pairs, axis=1))
+    )
     core_half = lax.all_gather(chip_pair, "z", axis=0, tiled=True)
     other_half = lax.ppermute(core_half, "c", [(0, 1), (1, 0)])
     half_rows = core_half.shape[0]
     proj_cols = query_cols + 2 * kv_cols
-    projected = jnp.dot(
+    own_part = jnp.dot(
         gathered[:, :half_rows], core_half[:, :proj_cols], preferred_element_type=jnp.float32
-    ) + jnp.dot(
+    )
+    own_part = lax.optimization_barrier(own_part)
+    projected = own_part + jnp.dot(
         gathered[:, half_rows:], other_half[:, :proj_cols], preferred_element_type=jnp.float32
     )
     position = positions_of(segment)

time: 210 us -> 217 us (1.033)
  starting transfers between devices: 24.4 us -> 31.6 us
    ppermute x1 -> x4, starting transfers between devices: 3.94 us -> 11.1 us  [layer(): pairs = tuple((lax.ppermute(w, 'xl', [(0, 1), (1, 0)]) for w in shards))]
  transfers between devices with their start and end apart: 5 -> 8, of which waited for: 4 -> 4; matrix products, arithmetic and copies ran while one was open for 6% -> 7% of each run, Pallas kernels for 0% -> 0%
where the time goes in v12:
time: 217 us; the launch traced here: 216 us
  waiting for transfers between devices  135 us (62%)
  starting transfers between devices  31.6 us (15%)
  other arithmetic  17.1 us (8%)
  between operations  14.3 us (7%)
  matrix products  11.1 us (5%)
  local copies, waits for them, and re-layouts  6.33 us (3%)
    all_gather x1, waiting for transfers between devices, layer(): core_half = lax.all_gather(chip_pair, 'z', axis=0, tiled=True)  78.9 us
    all_to_all x1, waiting for transfers between devices, layer(): lax.all_to_all(jnp.broadcast_to(normed[None], (tensor_size,) + normed.sha...  26.8 us
    all_to_all x1, waiting for transfers between devices, layer(): lax.all_to_all(out_rows.astype(jnp.bfloat16).reshape(tensor_size, -1, out...  26.4 us
    ppermute x4, starting transfers between devices, layer(): pairs = tuple((lax.ppermute(w, 'xl', [(0, 1), (1, 0)]) for w in shards))  11.1 us
    ppermute x1, starting transfers between devices, layer(): other_half = lax.ppermute(core_half, 'c', [(0, 1), (1, 0)])  10.1 us
    all_to_all x1, starting transfers between devices, layer(): lax.all_to_all(jnp.broadcast_to(normed[None], (tensor_size,) + normed.sha...  6.55 us
  transfers between devices with their start and end apart: 8, of which 4 were waited for; matrix products, arithmetic and copies ran while one was open for 7% of the time, Pallas kernels for 0%

profile of v12, /device:TPU:1, one launch (start us, length us, event | category | flops | bytes accessed | tf_op | source)
XLA Modules:
  0.0 215.9 jit_solution(16943906425957762270)
XLA Ops:
  7.2 3.9 %collective-permute-start.3 = (bf16[64,512]{1,0:T(8,128)(2,1)}, bf16[64,512]{1,0:T(8,128)(2,1)S(1)}, u32[]{:S(2)}, u32[]{:S(2)}) collective-permute-start(bf16[64,512]{1,0:T(8,128)(2,1)} %bitcast.88), channel_id=1, source_target_pairs={{0,16},{16,0},{1,17},{17,1},{2,18},{18,2},{3,19},{19,3},{4,20},{20... | collective-permute-start | bytes 196616 | tf_op jit(solution)/shard_map/ppermute | solution.py:79
  11.2 1.9 collective-permute-start
  13.1 3.4 %collective-permute-start.1 = (bf16[64,128]{1,0:T(8,128)(2,1)}, bf16[64,128]{1,0:T(8,128)(2,1)S(1)}, u32[]{:S(2)}, u32[]{:S(2)}) collective-permute-start(bf16[64,128]{1,0:T(8,128)(2,1)} %param.10), channel_id=1, source_target_pairs={{0,16},{16,0},{1,17},{17,1},{2,18},{18,2},{3,19},{19,3},{4,20},{20... | collective-permute-start | bytes 49160 | tf_op jit(solution)/shard_map/ppermute | solution.py:79
  16.5 1.9 collective-permute-start.2
  18.4 3.2 %collective-permute-done.2 = bf16[64,128]{1,0:T(8,128)(2,1)S(1)} collective-permute-done((bf16[64,128]{1,0:T(8,128)(2,1)}, bf16[64,128]{1,0:T(8,128)(2,1)S(1)}, u32[]{:S(2)}, u32[]{:S(2)}) %collective-permute-start.2) | collective-permute-done | bytes 16416 | tf_op jit(solution)/shard_map/ppermute | solution.py:79
  21.6 1.7 maximum_maximum_fusion
  23.3 78.9 %all-gather.2.cloned.1.call-done = bf16[2048,1280]{1,0:T(8,128)(2,1)} async-done(((bf16[128,1280]{1,0:T(8,128)(2,1)}), bf16[2048,1280]{1,0:T(8,128)(2,1)}) %all-gather.2.cloned.1.call-update) | async-done | bytes 5242896 | tf_op jit(solution)/shard_map/all_gather | solution.py:83
  102.2 10.1 %collective-permute-start.4 = (bf16[2048,1280]{1,0:T(8,128)(2,1)}, bf16[2048,1280]{1,0:T(8,128)(2,1)}, u32[]{:S(2)}, u32[]{:S(2)}) collective-permute-start(bf16[2048,1280]{1,0:T(8,128)(2,1)} %all-gather.2.cloned.1.call-done), channel_id=1, source_target_pairs={{0,8},{8,0},{1,9},{9,1},{2,10},{10,2},{3,11},{11,3},{4,12},{12,4},... | collective-permute-start | bytes 15728648 | tf_op jit(solution)/shard_map/ppermute | solution.py:84
  113.0 1.1 fusion.19
  114.1 1.1 fusion.21
  116.2 1.6 fusion.18
  117.8 2.3 %fusion.25 = bf16[32,2,16,2,64]{4,3,2,1,0:T(2,128)(2,1)S(1)} fusion(s32[]{:T(128)S(6)} %select_n.35, bf16[32,2,16,2,64]{4,3,2,1,0:T(2,128)(2,1)S(1)} %fusion.18), kind=kLoop, calls=%fused_computation.42 | loop fusion | flops 524288 | bytes 524292 | tf_op jit(solution)/shard_map/concatenate | solution.py:73
  120.5 1.5 broadcast_in_dim.16
  122.1 6.6 %all-to-all-start = ((bf16[8,32,4096]{2,1,0:T(8,128)(2,1)}), bf16[8,32,4096]{2,1,0:T(8,128)(2,1)S(1)}, u32[]{:S(2)}, u32[]{:S(2)}) async-start(bf16[8,32,4096]{2,1,0:T(8,128)(2,1)} %broadcast_in_dim.16), calls=%async_computation | async-start | bytes 4194304 | tf_op jit(solution)/shard_map/all_to_all | solution.py:75
  130.1 26.8 %all-to-all-done = bf16[8,32,4096]{2,1,0:T(8,128)(2,1)S(1)} async-done(((bf16[8,32,4096]{2,1,0:T(8,128)(2,1)}), bf16[8,32,4096]{2,1,0:T(8,128)(2,1)S(1)}, u32[]{:S(2)}, u32[]{:S(2)}) %all-to-all-start) | async-done | bytes 2097184 | tf_op jit(solution)/shard_map/all_to_all | solution.py:75
  156.9 2.9 %fusion.2 = f32[256,768]{1,0:T(8,128)S(1)} fusion(bf16[2048,1280]{1,0:T(8,128)(2,1)} %all-gather.2.cloned.1.call-done, bf16[256,4096]{1,0:T(8,128)(2,1)S(1)} %bitcast.82), kind=kOutput, calls=%fused_computation.3 | convolution fusion | flops 805306368 | bytes 4980736 | tf_op jit(solution)/shard_map/dot_general | solution.py:87
  159.7 2.9 %fusion.5 = f32[256,768]{1,0:T(8,128)S(1)} fusion(f32[256,768]{1,0:T(8,128)S(1)} %fusion.2, bf16[2048,1280]{1,0:T(8,128)(2,1)} %collective-permute-done.4, bf16[256,4096]{1,0:T(8,128)(2,1)S(1)} %bitcast.83), kind=kOutput, calls=%fused_computation.16 | convolution fusion | flops 805502976 | bytes 5767168 | tf_op jit(solution)/shard_map/dot_general | solution.py:91
  165.2 2.3 %convolution_convert_fusion.1 = bf16[8,32,2048]{2,1,0:T(8,128)(2,1)S(1)} fusion(bf16[8,32,512]{2,1,0:T(8,128)(2,1)S(1)} %dot_general.24, bf16[2048,1280]{1,0:T(8,128)(2,1)} %all-gather.2.cloned.1.call-done), kind=kOutput, calls=%fused_computation.6 | convolution fusion | flops 537395200 | bytes 3407872 | tf_op jit(solution)/shard_map/dot_general | solution.py:130
  167.6 2.3 %convolution_convert_fusion = bf16[8,32,2048]{2,1,0:T(8,128)(2,1)S(1)} fusion(bf16[8,32,512]{2,1,0:T(8,128)(2,1)S(1)} %dot_general.24, bf16[2048,1280]{1,0:T(8,128)(2,1)} %collective-permute-done.4), kind=kOutput, calls=%fused_computation.5 | convolution fusion | flops 537395200 | bytes 3407872 | tf_op jit(solution)/shard_map/dot_general | solution.py:131
  169.9 1.6 pad_maximum_fusion
  171.5 3.8 %all-to-all-start.1 = ((bf16[8,32,4096]{2,1,0:T(8,128)(2,1)}), bf16[8,32,4096]{2,1,0:T(8,128)(2,1)S(1)}, u32[]{:S(2)}, u32[]{:S(2)}) async-start(bf16[8,32,4096]{2,1,0:T(8,128)(2,1)} %pad_maximum_fusion), calls=%async_computation.1 | async-start | bytes 4194304 | tf_op jit(solution)/shard_map/all_to_all | solution.py:135
  176.0 26.4 %all-to-all-done.1 = bf16[8,32,4096]{2,1,0:T(8,128)(2,1)S(1)} async-done(((bf16[8,32,4096]{2,1,0:T(8,128)(2,1)}), bf16[8,32,4096]{2,1,0:T(8,128)(2,1)S(1)}, u32[]{:S(2)}, u32[]{:S(2)}) %all-to-all-start.1) | async-done | bytes 2097184 | tf_op jit(solution)/shard_map/all_to_all | solution.py:135
  203.4 1.1 fusion.13
  204.5 1.9 fusion.12
  (46 shorter events, 10.4 us)
Async XLA Ops:
  7.2 95.1 %all-gather.2.cloned.1.call-start = ((), (), s32[]{:S(2)}) async-start(), calls=%async_computation.2 | async-start | bytes 5570560 | tf_op jit(solution)/shard_map/all_gather | solution.py:83
  7.2 14.4 %collective-permute-start.3 = (bf16[64,512]{1,0:T(8,128)(2,1)}, bf16[64,512]{1,0:T(8,128)(2,1)S(1)}, u32[]{:S(2)}, u32[]{:S(2)}) collective-permute-start(bf16[64,512]{1,0:T(8,128)(2,1)} %bitcast.88), channel_id=1, source_target_pairs={{0,16},{16,0},{1,17},{17,1},{2,18},{18,2},{3,19},{19,3},{4,20},{20... | collective-permute-start | bytes 196616 | tf_op jit(solution)/shard_map/ppermute | solution.py:79
  11.2 10.5 %collective-permute-start = (bf16[64,512]{1,0:T(8,128)(2,1)}, bf16[64,512]{1,0:T(8,128)(2,1)S(1)}, u32[]{:S(2)}, u32[]{:S(2)}) collective-permute-start(bf16[64,512]{1,0:T(8,128)(2,1)} %param.9), channel_id=1, source_target_pairs={{0,16},{16,0},{1,17},{17,1},{2,18},{18,2},{3,19},{19,3},{4,20},{20... | collective-permute-start | bytes 196616 | tf_op jit(solution)/shard_map/ppermute | solution.py:79
  13.1 5.3 %collective-permute-start.1 = (bf16[64,128]{1,0:T(8,128)(2,1)}, bf16[64,128]{1,0:T(8,128)(2,1)S(1)}, u32[]{:S(2)}, u32[]{:S(2)}) collective-permute-start(bf16[64,128]{1,0:T(8,128)(2,1)} %param.10), channel_id=1, source_target_pairs={{0,16},{16,0},{1,17},{17,1},{2,18},{18,2},{3,19},{19,3},{4,20},{20... | collective-permute-start | bytes 49160 | tf_op jit(solution)/shard_map/ppermute | solution.py:79
  16.5 5.2 %collective-permute-start.2 = (bf16[64,128]{1,0:T(8,128)(2,1)}, bf16[64,128]{1,0:T(8,128)(2,1)S(1)}, u32[]{:S(2)}, u32[]{:S(2)}) collective-permute-start(bf16[64,128]{1,0:T(8,128)(2,1)} %param.11), channel_id=1, source_target_pairs={{0,16},{16,0},{1,17},{17,1},{2,18},{18,2},{3,19},{19,3},{4,20},{20... | collective-permute-start | bytes 49160 | tf_op jit(solution)/shard_map/ppermute | solution.py:79
  102.2 57.5 %collective-permute-start.4 = (bf16[2048,1280]{1,0:T(8,128)(2,1)}, bf16[2048,1280]{1,0:T(8,128)(2,1)}, u32[]{:S(2)}, u32[]{:S(2)}) collective-permute-start(bf16[2048,1280]{1,0:T(8,128)(2,1)} %all-gather.2.cloned.1.call-done), channel_id=1, source_target_pairs={{0,8},{8,0},{1,9},{9,1},{2,10},{10,2},{3,11},{11,3},{4,12},{12,4},... | collective-permute-start | bytes 15728648 | tf_op jit(solution)/shard_map/ppermute | solution.py:84
  122.1 6.6 %copy-start.1 = (s32[256]{0:T(256)S(1)}, s32[256]{0:T(256)}, u32[]{:S(2)}) copy-start(s32[256]{0:T(256)} %param.13) | copy-start | bytes 3076
  122.1 34.8 %all-to-all-start = ((bf16[8,32,4096]{2,1,0:T(8,128)(2,1)}), bf16[8,32,4096]{2,1,0:T(8,128)(2,1)S(1)}, u32[]{:S(2)}, u32[]{:S(2)}) async-start(bf16[8,32,4096]{2,1,0:T(8,128)(2,1)} %broadcast_in_dim.16), calls=%async_computation | async-start | bytes 4194304 | tf_op jit(solution)/shard_map/all_to_all | solution.py:75
  171.5 30.9 %all-to-all-start.1 = ((bf16[8,32,4096]{2,1,0:T(8,128)(2,1)}), bf16[8,32,4096]{2,1,0:T(8,128)(2,1)S(1)}, u32[]{:S(2)}, u32[]{:S(2)}) async-start(bf16[8,32,4096]{2,1,0:T(8,128)(2,1)} %pad_maximum_fusion), calls=%async_computation.1 | async-start | bytes 4194304 | tf_op jit(solution)/shard_map/all_to_all | solution.py:135
  206.4 1.8 copy-start
Sparse Core Ops, SparseCore 0:
  23.4 78.7 all-gather.1
